TPU v7x, 256 devices: a whole 4x4x8 slice. The times are simulated.
256 devices in a mesh: grp: 16 (over z, core), seq: 16 (over y, x).
Axes of the slice: x: 4, y: 4, z: 8, core: 2. Of those that a mesh axis runs over, the one named last changes fastest.
Arguments:
- query: bfloat16 [32, 8192], P('grp', 'seq'), may hold values from -16 to 16
- key_cache: bfloat16 [32, 16384, 1024], P('grp', 'seq'), may hold values from -64 to 64
- value_store_cache: bfloat16 [32, 16384, 1024], P('grp', 'seq'), may hold values from -6 to 6
- selected: int32 [32, 32], P('grp'), may hold values from 0 to 255, as said below
- lengths: int32 [32], P('grp'), may hold values from 2048 to 16384, as said below
- w_out: bfloat16 [8192, 8192], P('seq', 'grp'), may hold values from -0.0625 to 0.0625
Outputs:
- attended: bfloat16 [32, 8192], P('grp', 'seq')
- projected: bfloat16 [32, 8192], P('seq', 'grp')
Inputs may be any that keep to these rules, and one draw needn't show every extreme that they name: `selected`: each row lists 32 distinct page numbers in ascending order, all below ceil(lengths / 64), always including the page that holds position lengths - 1; recent pages are chosen more often. `lengths`: every length is at least 2048; some request has exactly 16384.
All inputs are finite; a program needn't handle non-finite values.
Results may differ from a plain program's by a relative error of at most 0.0056.
Values may be sent and summed in bfloat16 or wider, within the bound.
No kernel may reach another device: no remote copies, remote signals or barrier semaphores. Data moves between devices by JAX's collectives and lax.ppermute only.
A program may use at most 64 MiB of HBM per device.

v0:
```python
import jax
import jax.numpy as jnp
from jax import lax
from jax.sharding import PartitionSpec as P

HEAD_DIMENSION = 128
PAGE = 64


NEG = -1e30


def combined_all(value, axis, join):
    pieces = jax.tree.map(lambda part: lax.all_gather(part, axis), value)
    head = jax.tree.map(lambda part: part[0], pieces)
    tail = jax.tree.map(lambda part: part[1:], pieces)
    subtotal, _ = lax.scan(lambda subtotal, piece: (join(subtotal, piece), None), head, tail)
    return subtotal


def body(query, key_cache, value_store_cache, selected, lengths, w_out):
    nseq = lax.axis_size("seq")
    heads_all = lax.all_gather(query, "seq", axis=1, tiled=True)
    requests = query.shape[0]
    tok_local = key_cache.shape[1]
    kv_heads = key_cache.shape[2] // HEAD_DIMENSION
    q_heads = heads_all.shape[1] // HEAD_DIMENSION
    head_group = q_heads // kv_heads
    scale = HEAD_DIMENSION ** (-0.5)
    qgroup = heads_all.reshape(requests, kv_heads, head_group, HEAD_DIMENSION)
    first = lax.axis_index("seq") * tok_local
    positions = first + jnp.arange(tok_local)
    picked = jnp.any(selected[:, :, None] == (positions // PAGE)[None, None, :], axis=1)
    live = picked & (positions[None, :] < lengths[:, None])
    key_rows = key_cache.reshape(requests, tok_local, kv_heads, HEAD_DIMENSION)
    scores = (
        jnp.einsum("rkgd,rtkd->rkgt", qgroup, key_rows, preferred_element_type=jnp.float32) * scale
    )
    scores = jnp.where(live[:, None, None, :], scores, NEG)
    peak = jnp.max(scores, axis=-1)
    weights = jnp.where(live[:, None, None, :], jnp.exp(scores - peak[..., None]), 0.0)
    total = jnp.sum(weights, axis=-1)
    values = value_store_cache.reshape(requests, tok_local, kv_heads, HEAD_DIMENSION)
    accum = jnp.einsum(
        "rkgt,rtkd->rkgd", weights.astype(jnp.bfloat16), values, preferred_element_type=jnp.float32
    )
    peak = peak.reshape(requests, q_heads)
    total = total.reshape(requests, q_heads)
    accum = accum.reshape(requests, q_heads, HEAD_DIMENSION)
    heads_dev = q_heads // nseq

    def combine_parts(left, right):
        upper = jnp.maximum(left[0], right[0])
        left_f = jnp.exp(left[0] - upper)
        right_f = jnp.exp(right[0] - upper)
        return (
            upper,
            left[1] * left_f + right[1] * right_f,
            left[2] * left_f[..., None] + right[2] * right_f[..., None],
        )

    whole_max, whole_total, whole_accum = combined_all((peak, total, accum), "seq", combine_parts)
    own_accum = lax.dynamic_slice_in_dim(
        whole_accum, lax.axis_index("seq") * heads_dev, heads_dev, 1
    )
    own_total = lax.dynamic_slice_in_dim(
        whole_total, lax.axis_index("seq") * heads_dev, heads_dev, 1
    )
    attended = (
        (own_accum / own_total[..., None])
        .reshape(requests, heads_dev * HEAD_DIMENSION)
        .astype(jnp.bfloat16)
    )
    everyone = lax.all_gather(attended, "grp", axis=0, tiled=True)
    projected = lax.psum_scatter(
        jnp.dot(everyone, w_out, preferred_element_type=jnp.float32),
        "seq",
        scatter_dimension=0,
        tiled=True,
    ).astype(jnp.bfloat16)
    return (attended, projected)


def solution(mesh):
    return jax.shard_map(
        body,
        mesh=mesh,
        in_specs=(
            P("grp", "seq"),
            P("grp", "seq", None),
            P("grp", "seq", None),
            P("grp", None),
            P("grp"),
            P("seq", "grp"),
        ),
        out_specs=(P("grp", "seq"), P("seq", "grp")),
        check_vma=False,
    )
```

profile of v0, /device:TPU:0, one launch (start us, length us, event | category | flops | bytes accessed | tf_op | source)
XLA Modules:
  0.0 187.3 jit_solution(10890924312885867727)
XLA Ops:
  7.2 0.0 copy-start
  7.2 0.0 all-gather.3.cloned.1.call-start
  7.2 0.0 copy-start.1
  7.3 22.2 %all_gather.15 = bf16[2,8192]{1,0:T(2,128)(2,1)S(1)} all-gather(bf16[2,512]{1,0:T(2,128)(2,1)} %param.8), channel_id=1, replica_groups=mesh['grp'=16,'seq'=16] {'seq'}, dimensions={1}, use_global_device_ids=true | all-gather | bytes 34816 | tf_op jit(solution)/shard_map/all_gather | solution.py:23
  29.5 0.8 compare_reduce_fusion
  30.3 0.7 compare_and_fusion
  31.0 0.0 copy-start.2
  31.1 3.5 %fusion.32 = (f32[2,8,8]{2,1,0:T(8,128)S(1)}, f32[2,8,8,1024]{3,2,1,0:T(8,128)S(1)}) fusion(bf16[1,2,64,128]{3,1,2,0:T(2,128)(2,1)S(1)} %bitcast.64, pred[2,1024]{1,0:T(4,128)(4,1)S(1)} %compare_and_fusion, bf16[2,1024,1024]{2,1,0:T(8,128)(2,1)} %param.9), kind=kOutput, calls=%fused_computation.46 | convolution fusion | flops 33947520 | bytes 4753920 | tf_op jit(solution)/shard_map/rkgd,rtkd->rkgt/dot_general | solution.py:37
  34.5 0.0 copy-done.1
  34.5 1.6 fusion.15
  36.2 0.0 all-gather.3.cloned.1.call-update
  36.2 0.1 all_gather_reshape.9
  36.3 0.2 fusion.19
  36.5 0.1 all_gather_reshape.10
  36.6 22.7 %all_gather.16 = f32[16,2,64]{2,1,0:T(2,128)S(1)} all-gather(f32[1,2,64]{2,1,0:T(2,128)S(1)} %all_gather_reshape.9), channel_id=1, replica_groups=mesh['grp'=16,'seq'=16] {'seq'}, dimensions={0}, use_global_device_ids=true | all-gather | bytes 8704 | tf_op jit(solution)/shard_map/all_gather | solution.py:14
  59.3 21.1 %all_gather.17 = f32[16,2,64]{2,1,0:T(2,128)S(1)} all-gather(f32[1,2,64]{2,1,0:T(2,128)S(1)} %all_gather_reshape.10), channel_id=1, replica_groups=mesh['grp'=16,'seq'=16] {'seq'}, dimensions={0}, use_global_device_ids=true | all-gather | bytes 8704 | tf_op jit(solution)/shard_map/all_gather | solution.py:14
  80.4 0.0 copy-done.2
  80.4 0.6 dynamic-slice
  81.7 3.0 %all-gather.3.cloned.1.call-done = f32[16,2,64,128]{3,2,1,0:T(8,128)} async-done(((f32[1,2,64,128]{3,2,1,0:T(8,128)}), f32[16,2,64,128]{3,2,1,0:T(8,128)}) %all-gather.3.cloned.1.call-update) | async-done | bytes 1048592 | tf_op jit(solution)/shard_map/all_gather | solution.py:14
  84.7 0.8 slice_bitcast_fusion
  85.5 1.3 slice.29
  86.8 2.4 %while.14 = (s32[]{:T(128)}, f32[2,64]{1,0:T(2,128)S(1)}, f32[2,64]{1,0:T(2,128)S(1)}, f32[2,64,128]{2,1,0:T(8,128)S(1)}, f32[15,2,64]{2,1,0:T(2,128)S(1)}, /*in...) while((s32[]{:T(128)}, f32[2,64]{1,0:T(2,128)S(1)}, f32[2,64]{1,0:T(2,128)S(1)}, ...), condition=%wide.region_4.5_spmd, body=%wide.region_3.4_spmd.sunk | while | flops 49922 | bytes 201829 | solution.py:17
  86.8 0.1 fusion.42
  87.0 0.1 fusion.42
  87.2 0.1 fusion.42
  87.3 0.1 fusion.42
  87.5 0.1 fusion.42
  87.6 0.1 fusion.42
  87.8 0.1 fusion.42
  88.0 0.1 fusion.42
  88.1 0.1 fusion.42
  88.3 0.1 fusion.42
  88.4 0.1 fusion.42
  88.6 0.1 fusion.42
  88.7 0.1 fusion.42
  88.9 0.1 fusion.42
  89.1 0.1 fusion.42
  89.2 0.1 constant_dynamic-slice_fusion.1
  89.3 0.1 fusion.36
  89.4 0.1 fusion.28
  89.4 0.6 copy.41
  90.0 17.5 %all-gather = bf16[16,2,512]{2,1,0:T(2,128)(2,1)S(1)} all-gather(bf16[1,2,512]{2,1,0:T(2,128)(2,1)S(1)} %reshape.72), channel_id=1, replica_groups=mesh['grp'=16,'seq'=16] {'grp'}, dimensions={0}, use_global_device_ids=true | all-gather | bytes 34816 | tf_op jit(solution)/shard_map/all_gather | solution.py:74
  107.5 0.0 copy-done
  107.5 0.2 fusion.33
  107.7 72.2 %all-reduce = bf16[32,512]{1,0:T(8,128)(2,1)S(1)} all-reduce(f32[32,512]{1,0:T(8,128)S(1)} %fusion.33), channel_id=2, replica_groups=mesh['grp'=16,'seq'=16] {'seq'}, use_global_device_ids=true, to_apply=%region_5.6.clone | all-reduce | flops 16384 | bytes 98304
  179.9 0.6 dynamic-slice_convert_fusion
  (23 shorter events, 0.4 us)
Async XLA Ops:
  7.2 100.4 %copy-start = (bf16[512,512]{1,0:T(8,128)(2,1)S(1)}, bf16[512,512]{1,0:T(8,128)(2,1)}, u32[]{:S(2)}) copy-start(bf16[512,512]{1,0:T(8,128)(2,1)} %param.13) | copy-start | bytes 1572868
  7.2 77.5 %all-gather.3.cloned.1.call-start = ((), (), s32[]{:S(2)}) async-start(), calls=%async_computation | async-start | bytes 1114112 | tf_op jit(solution)/shard_map/all_gather | solution.py:14
  7.2 27.3 %copy-start.1 = (bf16[2,1024,1024]{2,1,0:T(8,128)(2,1)S(1)}, bf16[2,1024,1024]{2,1,0:T(8,128)(2,1)}, u32[]{:S(2)}) copy-start(bf16[2,1024,1024]{2,1,0:T(8,128)(2,1)} %param.10) | copy-start | bytes 12582916
  31.0 49.4 %copy-start.2 = (u32[256]{0:T(256)S(1)}, u32[256]{0:T(256)}, u32[]{:S(2)}) copy-start(u32[256]{0:T(256)} %constant.53) | copy-start | bytes 3076
Sparse Core Ops, SparseCore 0:
  36.3 48.3 all-gather.2
where the time goes:
time: 188 us; the launch traced here: 187 us
  blocking collectives  156 us (83%)
  between operations  14.8 us (8%)
  matrix products  5.28 us (3%)
  local copies, waits for them, and re-layouts  4.16 us (2%)
  other arithmetic  3.98 us (2%)
  waiting for transfers between devices  3 us (2%)
    unnamed x1, blocking collectives  72.2 us
    all_gather x2, blocking collectives, combined_all(): pieces = jax.tree.map(lambda part: lax.all_gather(part, axis), value)  43.9 us
    all_gather x1, blocking collectives, body(): heads_all = lax.all_gather(query, 'seq', axis=1, tiled=True)  22.2 us
    all_gather x1, blocking collectives, body(): everyone = lax.all_gather(attended, 'grp', axis=0, tiled=True)  17.5 us
  transfers between devices with their start and end apart: 1, of which 1 were waited for; matrix products, arithmetic and copies ran while one was open for 1% of the time, Pallas kernels for 0%

commit v1 on v0

v1 whole, which is shorter than its diff:
```python
import jax
import jax.numpy as jnp
from jax import lax
from jax.sharding import PartitionSpec as P

HEAD_DIMENSION = 128
PAGE = 64


NEG = -1e30


def gather_by_all_to_all(x, axis):
    n = lax.axis_size(axis)
    return lax.all_to_all(jnp.broadcast_to(x[None], (n,) + x.shape), axis, 0, 0, tiled=True)


def body(query, key_cache, value_store_cache, selected, lengths, w_out):
    nseq = lax.axis_size("seq")
    me = lax.axis_index("seq")
    requests = query.shape[0]
    tok_local = key_cache.shape[1]
    kv_heads = key_cache.shape[2] // HEAD_DIMENSION
    heads_dev = query.shape[1] // HEAD_DIMENSION
    q_heads = heads_dev * nseq
    head_group = q_heads // kv_heads
    scale = HEAD_DIMENSION ** (-0.5)

    heads_all = gather_by_all_to_all(query, "seq")
    qgroup = jnp.transpose(heads_all, (1, 0, 2)).reshape(requests, kv_heads, head_group, HEAD_DIMENSION)

    pages_local = tok_local // PAGE
    first_page = me * pages_local
    page_ids = first_page + jnp.arange(pages_local, dtype=jnp.int32)
    page_picked = jnp.any(selected[:, :, None] == page_ids[None, None, :], axis=1)
    positions = me * tok_local + jnp.arange(tok_local, dtype=jnp.int32)
    live = jnp.repeat(page_picked, PAGE, axis=1) & (positions[None, :] < lengths[:, None])

    key_rows = key_cache.reshape(requests, tok_local, kv_heads, HEAD_DIMENSION)
    scores = (
        jnp.einsum("rkgd,rtkd->rkgt", qgroup, key_rows, preferred_element_type=jnp.float32) * scale
    )
    scores = jnp.where(live[:, None, None, :], scores, NEG)
    peak = jnp.max(scores, axis=-1)
    weights = jnp.where(live[:, None, None, :], jnp.exp(scores - peak[..., None]), 0.0)
    total = jnp.sum(weights, axis=-1)
    values = value_store_cache.reshape(requests, tok_local, kv_heads, HEAD_DIMENSION)
    accum = jnp.einsum(
        "rkgt,rtkd->rkgd", weights.astype(jnp.bfloat16), values, preferred_element_type=jnp.float32
    )
    packed = jnp.concatenate(
        [
            accum.reshape(requests, q_heads, HEAD_DIMENSION),
            peak.reshape(requests, q_heads, 1),
            total.reshape(requests, q_heads, 1),
        ],
        axis=-1,
    )
    packed = jnp.transpose(
        packed.reshape(requests, nseq, heads_dev, HEAD_DIMENSION + 2), (1, 0, 2, 3)
    )
    parts = lax.all_to_all(packed, "seq", 0, 0, tiled=True)
    b_out = parts[..., :HEAD_DIMENSION]
    b_max = parts[..., HEAD_DIMENSION]
    b_sum = parts[..., HEAD_DIMENSION + 1]
    top = jnp.max(b_max, axis=0)
    factor = jnp.exp(b_max - top[None])
    whole_total = jnp.sum(b_sum * factor, axis=0)
    whole_accum = jnp.sum(b_out * factor[..., None], axis=0)
    attended = (
        (whole_accum / whole_total[..., None])
        .reshape(requests, heads_dev * HEAD_DIMENSION)
        .astype(jnp.bfloat16)
    )
    everyone = gather_by_all_to_all(attended, "grp").reshape(-1, attended.shape[1])
    partial = jnp.dot(everyone, w_out, preferred_element_type=jnp.float32)
    partial = partial.reshape(nseq, -1, partial.shape[1])
    pieces = lax.all_to_all(partial, "seq", 0, 0, tiled=True)
    projected = jnp.sum(pieces, axis=0).astype(jnp.bfloat16)
    return (attended, projected)


def solution(mesh):
    return jax.shard_map(
        body,
        mesh=mesh,
        in_specs=(
            P("grp", "seq"),
            P("grp", "seq", None),
            P("grp", "seq", None),
            P("grp", None),
            P("grp"),
            P("seq", "grp"),
        ),
        out_specs=(P("grp", "seq"), P("seq", "grp")),
        check_vma=False,
    )
```

time: 188 us -> 64.2 us (0.34)
  the two profiles are of different devices: /device:TPU:0 before, /device:TPU:1 now
where the time goes in v1:
time: 64.2 us; the launch traced here: 63.8 us
  blocking collectives  38.1 us (59%)
  starting transfers between devices  7.57 us (12%)
  matrix products  6.81 us (11%)
  waiting for transfers between devices  4.68 us (7%)
  other arithmetic  3.13 us (5%)
  local copies, waits for them, and re-layouts  2.78 us (4%)
  between operations  0.72 us (1%)
    all_to_all x1, blocking collectives, gather_by_all_to_all(): lax.all_to_all(jnp.broadcast_to(x[None], (n,) + x.shape), axis, 0, 0, til...  18.9 us
    all_to_all x1, blocking collectives, body(): parts = lax.all_to_all(packed, 'seq', 0, 0, tiled=True)  9.9 us
    all_to_all x1, blocking collectives, body(): pieces = lax.all_to_all(partial, 'seq', 0, 0, tiled=True)  9.31 us
    all_to_all x1, starting transfers between devices, gather_by_all_to_all(): lax.all_to_all(jnp.broadcast_to(x[None], (n,) + x.shape), axis, 0, 0, til...  7.57 us
    all_to_all x1, waiting for transfers between devices, gather_by_all_to_all(): lax.all_to_all(jnp.broadcast_to(x[None], (n,) + x.shape), axis, 0, 0, til...  4.68 us
    dot_general x1, matrix products, body(): jnp.einsum('rkgd,rtkd->rkgt', qgroup, key_rows, preferred_element_type=jn...  3.46 us
    dot_general x1, matrix products, body(): jnp.einsum('rkgt,rtkd->rkgd', weights.astype(jnp.bfloat16), values, prefe...  3.17 us
    broadcast_in_dim x2, local copies, waits for them, and re-layouts, gather_by_all_to_all(): jnp.broadcast_to(x[None], (n,) + x.shape)  1.38 us
  transfers between devices with their start and end apart: 1, of which 1 were waited for; matrix products, arithmetic and copies ran while one was open for 3% of the time, Pallas kernels for 0%

profile of v1, /device:TPU:1, one launch (start us, length us, event | category | flops | bytes accessed | tf_op | source)
XLA Modules:
  0.0 63.8 jit_solution(7459364253188327273)
XLA Ops:
  0.6 0.0 copy-start
  0.6 1.4 %broadcast_in_dim.26 = bf16[16,2,512]{2,1,0:T(2,128)(2,1)} broadcast(bf16[2,512]{1,0:T(2,128)(2,1)} %param.6), dimensions={1,2} | broadcast | bytes 34816 | tf_op jit(solution)/shard_map/broadcast_in_dim | solution.py:15
  2.0 7.6 %all-to-all-start = ((bf16[16,2,512]{2,1,0:T(2,128)(2,1)}), bf16[16,2,512]{2,1,0:T(2,128)(2,1)S(1)}, u32[]{:S(2)}, u32[]{:S(2)}) async-start(bf16[16,2,512]{2,1,0:T(2,128)(2,1)} %broadcast_in_dim.26), calls=%async_computation | async-start | bytes 65536 | tf_op jit(solution)/shard_map/all_to_all | solution.py:15
  9.6 0.9 %compare_reduce_fusion = pred[2,16]{1,0:T(4,128)(4,1)S(1)} fusion(s32[2,32]{1,0:T(2,128)} %param.9, s32[16]{0:T(128)S(1)} %iota_add_fusion.1), kind=kLoop, calls=%fused_computation.21 | loop fusion | flops 2016 | bytes 352 | tf_op jit(solution)/shard_map/reduce_or | solution.py:35
  10.5 0.1 broadcast_in_dim.24
  10.5 0.1 reshape.86
  10.6 0.7 %compare_and_fusion = pred[2,1024]{1,0:T(4,128)(4,1)S(1)} fusion(pred[2,1024]{1,0:T(4,128)(4,1)S(1)} %reshape.86, s32[1024]{0:T(1024)S(1)} %iota_add_fusion, s32[2]{0:T(128)} %param.10), kind=kLoop, calls=%fused_computation.20 | loop fusion | flops 4096 | bytes 8200 | tf_op jit(solution)/shard_map/and | solution.py:37
  11.4 4.7 %all-to-all-done = bf16[16,2,512]{2,1,0:T(2,128)(2,1)S(1)} async-done(((bf16[16,2,512]{2,1,0:T(2,128)(2,1)}), bf16[16,2,512]{2,1,0:T(2,128)(2,1)S(1)}, u32[]{:S(2)}, u32[]{:S(2)}) %all-to-all-start) | async-done | bytes 32800 | tf_op jit(solution)/shard_map/all_to_all | solution.py:15
  16.1 3.5 %fusion.28 = (f32[2,8,8]{2,1,0:T(8,128)S(1)}, f32[2,8,8,1024]{3,2,1,0:T(8,128)S(1)}) fusion(bf16[2,8,8,128]{3,2,1,0:T(8,128)(2,1)S(1)} %reshape.87, pred[2,1024]{1,0:T(4,128)(4,1)S(1)} %compare_and_fusion, bf16[2,1024,1024]{2,1,0:T(8,128)(2,1)} %param.7), kind=kOutput, calls=%fused_computation.35 | convolution fusion | flops 33947520 | bytes 4753920 | tf_op jit(solution)/shard_map/rkgd,rtkd->rkgt/dot_general | solution.py:41
  19.6 0.1 concatenate.11
  19.6 0.2 fusion.14
  19.9 3.2 %fusion = f32[2,8,8,128]{3,2,1,0:T(8,128)S(1)} fusion(f32[2,8,8,1024]{3,2,1,0:T(8,128)S(1)} %get-tuple-element.6, f32[2,8,8]{2,1,0:T(8,128)S(1)} %get-tuple-element.5, pred[2,1024]{1,0:T(4,128)(4,1)S(1)} %compare_and_fusion, bf16[2,1024,1024]{2,1,0:T(8,128)(2,1)} %param.8), kind=kOutput, calls=%fused_computation | convolution fusion | flops 33947648 | bytes 4786688 | tf_op jit(solution)/shard_map/rkgt,rtkd->rkgd/dot_general | solution.py:48
  23.1 0.1 concatenate.12
  23.1 0.3 copy.66
  23.4 0.3 copy.65
  23.7 0.1 maximum_bitcast_fusion
  23.9 9.9 %all_to_all.20 = f32[16,2,4,130]{3,2,1,0:T(4,128)S(1)} all-to-all(f32[16,2,4,130]{3,2,1,0:T(4,128)S(1)} %maximum_bitcast_fusion), channel_id=1, replica_groups=mesh['grp'=16,'seq'=16] {'seq'}, dimensions={0} | all-to-all | bytes 133120 | tf_op jit(solution)/shard_map/all_to_all | solution.py:62
  33.8 0.1 fusion.27
  33.9 0.1 copy.70
  34.0 0.1 copy.75
  34.1 0.1 exponential_bitcast_fusion
  34.2 0.2 fusion.24
  34.4 0.1 copy.68
  34.5 0.1 fusion.20
  34.6 0.1 fusion.25
  34.7 0.0 copy-start.1
  34.7 18.9 %all_to_all.21 = bf16[16,2,512]{2,1,0:T(2,128)(2,1)S(1)} all-to-all(bf16[16,2,512]{2,1,0:T(2,128)(2,1)S(1)} %broadcast_in_dim.48), channel_id=1, replica_groups=mesh['grp'=16,'seq'=16] {'grp'}, dimensions={0} | all-to-all | bytes 65536 | tf_op jit(solution)/shard_map/all_to_all | solution.py:15
  53.6 0.0 copy-done
  53.6 0.2 fusion.12
  53.8 0.1 copy.73
  53.9 9.3 %all_to_all.22 = f32[16,2,512]{2,1,0:T(2,128)S(1)} all-to-all(f32[16,2,512]{2,1,0:T(2,128)S(1)} %copy.73), channel_id=1, replica_groups=mesh['grp'=16,'seq'=16] {'seq'}, dimensions={0} | all-to-all | bytes 131072 | tf_op jit(solution)/shard_map/all_to_all | solution.py:78
  63.2 0.6 reduce_sum.39
  63.8 0.0 copy-done.1
  (6 shorter events, 0.1 us)
Async XLA Ops:
  0.6 53.0 %copy-start = (bf16[512,512]{1,0:T(8,128)(2,1)S(1)}, bf16[512,512]{1,0:T(8,128)(2,1)}, u32[]{:S(2)}) copy-start(bf16[512,512]{1,0:T(8,128)(2,1)} %param.11) | copy-start | bytes 1572868
  2.0 14.1 %all-to-all-start = ((bf16[16,2,512]{2,1,0:T(2,128)(2,1)}), bf16[16,2,512]{2,1,0:T(2,128)(2,1)S(1)}, u32[]{:S(2)}, u32[]{:S(2)}) async-start(bf16[16,2,512]{2,1,0:T(2,128)(2,1)} %broadcast_in_dim.26), calls=%async_computation | async-start | bytes 65536 | tf_op jit(solution)/shard_map/all_to_all | solution.py:15
  34.7 29.1 %copy-start.1 = (bf16[1,2,4,128]{3,1,2,0:T(2,128)(2,1)}, bf16[1,2,4,128]{3,1,2,0:T(2,128)(2,1)S(1)}, u32[]{:S(2)}) copy-start(bf16[1,2,4,128]{3,1,2,0:T(2,128)(2,1)S(1)} %copy.99) | copy-start | bytes 6148

commit v2 on v1

--- a/solution.py
+++ b/solution.py
@@ -27,7 +27,6 @@
     scale = HEAD_DIMENSION ** (-0.5)
 
     heads_all = gather_by_all_to_all(query, "seq")
-    qgroup = jnp.transpose(heads_all, (1, 0, 2)).reshape(requests, kv_heads, head_group, HEAD_DIMENSION)
 
     pages_local = tok_local // PAGE
     first_page = me * pages_local
@@ -36,18 +35,22 @@
     positions = me * tok_local + jnp.arange(tok_local, dtype=jnp.int32)
     live = jnp.repeat(page_picked, PAGE, axis=1) & (positions[None, :] < lengths[:, None])
 
-    key_rows = key_cache.reshape(requests, tok_local, kv_heads, HEAD_DIMENSION)
+    own_kv = (jnp.arange(q_heads) // head_group)[:, None] == jnp.arange(kv_heads)[None, :]
+    qfull = jnp.transpose(heads_all, (1, 0, 2)).reshape(requests, q_heads, 1, HEAD_DIMENSION)
+    qdiag = jnp.where(own_kv[None, :, :, None], qfull, jnp.zeros((), qfull.dtype)).reshape(
+        requests, q_heads, kv_heads * HEAD_DIMENSION
+    )
     scores = (
-        jnp.einsum("rkgd,rtkd->rkgt", qgroup, key_rows, preferred_element_type=jnp.float32) * scale
+        jnp.einsum("rhc,rtc->rht", qdiag, key_cache, preferred_element_type=jnp.float32) * scale
     )
-    scores = jnp.where(live[:, None, None, :], scores, NEG)
+    scores = jnp.where(live[:, None, :], scores, NEG)
     peak = jnp.max(scores, axis=-1)
-    weights = jnp.where(live[:, None, None, :], jnp.exp(scores - peak[..., None]), 0.0)
+    weights = jnp.where(live[:, None, :], jnp.exp(scores - peak[..., None]), 0.0)
     total = jnp.sum(weights, axis=-1)
-    values = value_store_cache.reshape(requests, tok_local, kv_heads, HEAD_DIMENSION)
-    accum = jnp.einsum(
-        "rkgt,rtkd->rkgd", weights.astype(jnp.bfloat16), values, preferred_element_type=jnp.float32
-    )
+    full = jnp.einsum(
+        "rht,rtc->rhc", weights.astype(jnp.bfloat16), value_store_cache, preferred_element_type=jnp.float32
+    ).reshape(requests, q_heads, kv_heads, HEAD_DIMENSION)
+    accum = jnp.sum(jnp.where(own_kv[None, :, :, None], full, 0.0), axis=2)
     packed = jnp.concatenate(
         [
             accum.reshape(requests, q_heads, HEAD_DIMENSION),

time: 64.2 us -> 64.4 us (level)
  no operation moved by 1% of the time
where the time goes in v2:
time: 64.4 us; the launch traced here: 64 us
  blocking collectives  38.1 us (59%)
  starting transfers between devices  7.57 us (12%)
  matrix products  6.94 us (11%)
  waiting for transfers between devices  4.41 us (7%)
  other arithmetic  3.43 us (5%)
  local copies, waits for them, and re-layouts  2.78 us (4%)
  between operations  0.8 us (1%)
    all_to_all x1, blocking collectives, gather_by_all_to_all(): lax.all_to_all(jnp.broadcast_to(x[None], (n,) + x.shape), axis, 0, 0, til...  18.9 us
    all_to_all x1, blocking collectives, body(): parts = lax.all_to_all(packed, 'seq', 0, 0, tiled=True)  9.9 us
    all_to_all x1, blocking collectives, body(): pieces = lax.all_to_all(partial, 'seq', 0, 0, tiled=True)  9.31 us
    all_to_all x1, starting transfers between devices, gather_by_all_to_all(): lax.all_to_all(jnp.broadcast_to(x[None], (n,) + x.shape), axis, 0, 0, til...  7.57 us
    all_to_all x1, waiting for transfers between devices, gather_by_all_to_all(): lax.all_to_all(jnp.broadcast_to(x[None], (n,) + x.shape), axis, 0, 0, til...  4.41 us
    dot_general x1, matrix products, body(): jnp.einsum('rhc,rtc->rht', qdiag, key_cache, preferred_element_type=jnp.f...  3.67 us
    dot_general x1, matrix products, body(): jnp.einsum('rht,rtc->rhc', weights.astype(jnp.bfloat16), value_store_cach...  3.09 us
    broadcast_in_dim x2, local copies, waits for them, and re-layouts, gather_by_all_to_all(): jnp.broadcast_to(x[None], (n,) + x.shape)  1.38 us
  transfers between devices with their start and end apart: 1, of which 1 were waited for; matrix products, arithmetic and copies ran while one was open for 3% of the time, Pallas kernels for 0%

profile of v2, /device:TPU:1, one launch (start us, length us, event | category | flops | bytes accessed | tf_op | source)
XLA Modules:
  0.0 64.0 jit_solution(18370824919097763795)
XLA Ops:
  0.6 0.0 copy-start
  0.6 1.4 %broadcast_in_dim.93 = bf16[16,2,512]{2,1,0:T(2,128)(2,1)} broadcast(bf16[2,512]{1,0:T(2,128)(2,1)} %param.6), dimensions={1,2} | broadcast | bytes 34816 | tf_op jit(solution)/shard_map/broadcast_in_dim | solution.py:15
  2.0 7.6 %all-to-all-start = ((bf16[16,2,512]{2,1,0:T(2,128)(2,1)}), bf16[16,2,512]{2,1,0:T(2,128)(2,1)S(1)}, u32[]{:S(2)}, u32[]{:S(2)}) async-start(bf16[16,2,512]{2,1,0:T(2,128)(2,1)} %broadcast_in_dim.93), calls=%async_computation | async-start | bytes 65536 | tf_op jit(solution)/shard_map/all_to_all | solution.py:15
  9.6 0.9 %compare_reduce_fusion = pred[2,16]{1,0:T(4,128)(4,1)S(1)} fusion(s32[2,32]{1,0:T(2,128)} %param.9, s32[16]{0:T(128)S(1)} %iota_add_fusion.1), kind=kLoop, calls=%fused_computation.23 | loop fusion | flops 2016 | bytes 352 | tf_op jit(solution)/shard_map/reduce_or | solution.py:34
  10.5 0.1 broadcast_in_dim.88
  10.6 0.1 reshape.118
  10.7 0.7 %compare_and_fusion = pred[2,1024]{1,0:T(4,128)(4,1)S(1)} fusion(pred[2,1024]{1,0:T(4,128)(4,1)S(1)} %reshape.118, s32[1024]{0:T(1024)S(1)} %iota_add_fusion, s32[2]{0:T(128)} %param.10), kind=kLoop, calls=%fused_computation.22 | loop fusion | flops 4096 | bytes 8200 | tf_op jit(solution)/shard_map/and | solution.py:36
  11.4 0.1 iota_compare_fusion
  11.5 0.1 broadcast_in_dim.90
  11.6 4.4 %all-to-all-done = bf16[16,2,512]{2,1,0:T(2,128)(2,1)S(1)} async-done(((bf16[16,2,512]{2,1,0:T(2,128)(2,1)}), bf16[16,2,512]{2,1,0:T(2,128)(2,1)S(1)}, u32[]{:S(2)}, u32[]{:S(2)}) %all-to-all-start) | async-done | bytes 32800 | tf_op jit(solution)/shard_map/all_to_all | solution.py:15
  16.1 0.1 broadcast_in_dim.96
  16.3 3.7 %fusion.23 = (f32[2,64]{1,0:T(2,128)S(1)}, f32[2,64,1024]{2,1,0:T(8,128)S(1)}) fusion(bf16[2,1024,1024]{2,1,0:T(8,128)(2,1)} %param.7, bf16[2,64,1024]{2,1,0:T(8,128)(2,1)S(1)} %broadcast_in_dim.96, pred[64,1024]{1,0:T(8,128)(4,1)S(1)} %bitcast.42, pred[2,1024]{1,0:T(4,128)(4,1)S(1)} %compare_and_fusion), kind=kOutput, calls=%fused_computation.42 | convolution fusion | flops 268959616 | bytes 5048832 | tf_op jit(solution)/shard_map/rhc,rtc->rht/dot_general | solution.py:44
  19.9 0.2 concatenate.14
  20.1 0.2 fusion.4
  20.4 3.1 %fusion.6 = f32[2,64,1024]{2,1,0:T(8,128)S(1)} fusion(bf16[2,1024,1024]{2,1,0:T(8,128)(2,1)} %param.8, f32[2,64,1024]{2,1,0:T(8,128)S(1)} %get-tuple-element.6, f32[2,64]{1,0:T(2,128)S(1)} %get-tuple-element.5, pred[2,1024]{1,0:T(4,128)(4,1)S(1)} %compare_and_fusion), kind=kOutput, calls=%fused_computation.9 | convolution fusion | flops 268828672 | bytes 5245440 | tf_op jit(solution)/shard_map/rht,rtc->rhc/dot_general | solution.py:50
  23.4 0.1 copy.57
  23.6 0.2 fusion.1
  23.8 0.2 concatenate.15
  24.0 0.1 maximum_bitcast_fusion
  24.1 9.9 %all_to_all.20 = f32[16,2,4,130]{3,2,1,0:T(4,128)S(1)} all-to-all(f32[16,2,4,130]{3,2,1,0:T(4,128)S(1)} %copy.48), channel_id=1, replica_groups=mesh['grp'=16,'seq'=16] {'seq'}, dimensions={0} | all-to-all | bytes 133120 | tf_op jit(solution)/shard_map/all_to_all | solution.py:65
  34.0 0.1 fusion.22
  34.1 0.1 copy.51
  34.2 0.1 copy.54
  34.4 0.1 exponential_bitcast_fusion
  34.4 0.2 fusion.18
  34.6 0.1 copy.50
  34.7 0.1 fusion.14
  34.8 0.1 fusion.19
  34.9 0.0 copy-start.1
  34.9 18.9 %all_to_all.21 = bf16[16,2,512]{2,1,0:T(2,128)(2,1)S(1)} all-to-all(bf16[16,2,512]{2,1,0:T(2,128)(2,1)S(1)} %broadcast_in_dim.101), channel_id=1, replica_groups=mesh['grp'=16,'seq'=16] {'grp'}, dimensions={0} | all-to-all | bytes 65536 | tf_op jit(solution)/shard_map/all_to_all | solution.py:15
  53.8 0.0 copy-done
  53.9 0.2 fusion.2
  54.0 0.1 copy.53
  54.1 9.3 %all_to_all.22 = f32[16,2,512]{2,1,0:T(2,128)S(1)} all-to-all(f32[16,2,512]{2,1,0:T(2,128)S(1)} %copy.53), channel_id=1, replica_groups=mesh['grp'=16,'seq'=16] {'seq'}, dimensions={0} | all-to-all | bytes 131072 | tf_op jit(solution)/shard_map/all_to_all | solution.py:81
  63.4 0.6 reduce_sum.49
  64.0 0.0 copy-done.1
  (10 shorter events, 0.2 us)
Async XLA Ops:
  0.6 53.2 %copy-start = (bf16[512,512]{1,0:T(8,128)(2,1)S(1)}, bf16[512,512]{1,0:T(8,128)(2,1)}, u32[]{:S(2)}) copy-start(bf16[512,512]{1,0:T(8,128)(2,1)} %param.11) | copy-start | bytes 1572868
  2.0 14.1 %all-to-all-start = ((bf16[16,2,512]{2,1,0:T(2,128)(2,1)}), bf16[16,2,512]{2,1,0:T(2,128)(2,1)S(1)}, u32[]{:S(2)}, u32[]{:S(2)}) async-start(bf16[16,2,512]{2,1,0:T(2,128)(2,1)} %broadcast_in_dim.93), calls=%async_computation | async-start | bytes 65536 | tf_op jit(solution)/shard_map/all_to_all | solution.py:15
  34.9 29.1 %copy-start.1 = (bf16[1,2,4,128]{3,1,2,0:T(2,128)(2,1)}, bf16[1,2,4,128]{3,1,2,0:T(2,128)(2,1)S(1)}, u32[]{:S(2)}) copy-start(bf16[1,2,4,128]{3,1,2,0:T(2,128)(2,1)S(1)} %copy.64) | copy-start | bytes 6148

commit v3 on v2

--- a/solution.py
+++ b/solution.py
@@ -1,6 +1,9 @@
+import functools
+
 import jax
 import jax.numpy as jnp
 from jax import lax
+from jax.experimental import pallas as pl
 from jax.sharding import PartitionSpec as P
 
 HEAD_DIMENSION = 128
@@ -13,6 +16,54 @@
 def gather_by_all_to_all(x, axis):
     n = lax.axis_size(axis)
     return lax.all_to_all(jnp.broadcast_to(x[None], (n,) + x.shape), axis, 0, 0, tiled=True)
+
+
+def attention_kernel(q_ref, live_ref, k_ref, v_ref, acc_ref, stat_ref, *, scale, head_group):
+    q = q_ref[0]
+    live = live_ref[0] > 0
+    scores = lax.dot_general(
+        q, k_ref[0], (((1,), (1,)), ((), ())), preferred_element_type=jnp.float32
+    ) * scale
+    scores = jnp.where(live, scores, NEG)
+    peak = jnp.max(scores, axis=-1, keepdims=True)
+    weights = jnp.where(live, jnp.exp(scores - peak), 0.0)
+    total = jnp.sum(weights, axis=-1, keepdims=True)
+    full = jnp.dot(weights.astype(jnp.bfloat16), v_ref[0], preferred_element_type=jnp.float32)
+    q_heads = q.shape[0]
+    for kv in range(q_heads // head_group):
+        rows = slice(kv * head_group, (kv + 1) * head_group)
+        acc_ref[0, rows, :] = full[rows, kv * HEAD_DIMENSION:(kv + 1) * HEAD_DIMENSION]
+    lane = lax.broadcasted_iota(jnp.int32, stat_ref.shape[1:], 1)
+    stat_ref[0] = jnp.where(lane == 0, peak, jnp.where(lane == 1, total, 0.0))
+
+
+def attention(qdiag, live, key_cache, value_store_cache, scale, head_group):
+    requests, q_heads, width = qdiag.shape
+    tok = key_cache.shape[1]
+    kernel = functools.partial(attention_kernel, scale=scale, head_group=head_group)
+    flops = 4 * requests * q_heads * tok * width
+    nbytes = 2 * (key_cache.size + value_store_cache.size + qdiag.size)
+    return pl.pallas_call(
+        kernel,
+        grid=(requests,),
+        in_specs=[
+            pl.BlockSpec((1, q_heads, width), lambda r: (r, 0, 0)),
+            pl.BlockSpec((1, 1, tok), lambda r: (r, 0, 0)),
+            pl.BlockSpec((1, tok, width), lambda r: (r, 0, 0)),
+            pl.BlockSpec((1, tok, width), lambda r: (r, 0, 0)),
+        ],
+        out_specs=[
+            pl.BlockSpec((1, q_heads, HEAD_DIMENSION), lambda r: (r, 0, 0)),
+            pl.BlockSpec((1, q_heads, HEAD_DIMENSION), lambda r: (r, 0, 0)),
+        ],
+        out_shape=[
+            jax.ShapeDtypeStruct((requests, q_heads, HEAD_DIMENSION), jnp.float32),
+            jax.ShapeDtypeStruct((requests, q_heads, HEAD_DIMENSION), jnp.float32),
+        ],
+        cost_estimate=pl.CostEstimate(
+            flops=flops, transcendentals=requests * q_heads * tok, bytes_accessed=nbytes
+        ),
+    )(qdiag, live.astype(jnp.int32).reshape(requests, 1, tok), key_cache, value_store_cache)
 
 
 def body(query, key_cache, value_store_cache, selected, lengths, w_out):
@@ -40,17 +91,9 @@
     qdiag = jnp.where(own_kv[None, :, :, None], qfull, jnp.zeros((), qfull.dtype)).reshape(
         requests, q_heads, kv_heads * HEAD_DIMENSION
     )
-    scores = (
-        jnp.einsum("rhc,rtc->rht", qdiag, key_cache, preferred_element_type=jnp.float32) * scale
-    )
-    scores = jnp.where(live[:, None, :], scores, NEG)
-    peak = jnp.max(scores, axis=-1)
-    weights = jnp.where(live[:, None, :], jnp.exp(scores - peak[..., None]), 0.0)
-    total = jnp.sum(weights, axis=-1)
-    full = jnp.einsum(
-        "rht,rtc->rhc", weights.astype(jnp.bfloat16), value_store_cache, preferred_element_type=jnp.float32
-    ).reshape(requests, q_heads, kv_heads, HEAD_DIMENSION)
-    accum = jnp.sum(jnp.where(own_kv[None, :, :, None], full, 0.0), axis=2)
+    accum, stats = attention(qdiag, live, key_cache, value_store_cache, scale, head_group)
+    peak = stats[..., 0]
+    total = stats[..., 1]
     packed = jnp.concatenate(
         [
             accum.reshape(requests, q_heads, HEAD_DIMENSION),

time: 64.4 us -> 63.8 us (level)
  matrix products: 6.94 us -> 0.18 us
  Pallas kernels: 0 us -> 5.52 us
  other arithmetic: 3.43 us -> 5.04 us
    dot_general x2 -> x0, matrix products: 6.75 us -> none  [the longest x1 3.67 us: body(): jnp.einsum('rhc,rtc->rht', qdiag, key_cache, preferred_element_type=jnp.f...]
    pallas_call x0 -> x1, Pallas kernels: none -> 5.52 us  [attention(): pl.pallas_call(kernel, grid=(requests,), in_specs=[pl.BlockSpec((1, q_hea...]
    convert_element_type x0 -> x1, other arithmetic: none -> 1.33 us  [attention(): live.astype(jnp.int32).reshape(requests, 1, tok)]
    concatenate x0 -> x1, other arithmetic: none -> 0.88 us  [body(): jnp.concatenate([accum.reshape(requests, q_heads, HEAD_DIMENSION), peak.r...]
    and x1 -> x0, other arithmetic: 0.73 us -> none  [body(): jnp.repeat(page_picked, PAGE, axis=1)]
    select_n x0 -> x1, other arithmetic: none -> 0.72 us  [body(): jnp.where(own_kv[None, :, :, None], qfull, jnp.zeros((), qfull.dtype))]
  transfers between devices with their start and end apart: 1 -> 1, of which waited for: 1 -> 1; matrix products, arithmetic and copies ran while one was open for 3% -> 4% of each run, Pallas kernels for 0% -> 0%
where the time goes in v3:
time: 63.8 us; the launch traced here: 63.4 us
  blocking collectives  38.1 us (60%)
  starting transfers between devices  7.57 us (12%)
  Pallas kernels  5.52 us (9%)
  other arithmetic  5.04 us (8%)
  waiting for transfers between devices  3.82 us (6%)
  local copies, waits for them, and re-layouts  2.4 us (4%)
  between operations  0.76 us (1%)
    all_to_all x1, blocking collectives, gather_by_all_to_all(): lax.all_to_all(jnp.broadcast_to(x[None], (n,) + x.shape), axis, 0, 0, til...  18.9 us
    all_to_all x1, blocking collectives, body(): parts = lax.all_to_all(packed, 'seq', 0, 0, tiled=True)  9.9 us
    all_to_all x1, blocking collectives, body(): pieces = lax.all_to_all(partial, 'seq', 0, 0, tiled=True)  9.31 us
    all_to_all x1, starting transfers between devices, gather_by_all_to_all(): lax.all_to_all(jnp.broadcast_to(x[None], (n,) + x.shape), axis, 0, 0, til...  7.57 us
    pallas_call x1, Pallas kernels, attention(): pl.pallas_call(kernel, grid=(requests,), in_specs=[pl.BlockSpec((1, q_hea...  5.52 us
    all_to_all x1, waiting for transfers between devices, gather_by_all_to_all(): lax.all_to_all(jnp.broadcast_to(x[None], (n,) + x.shape), axis, 0, 0, til...  3.82 us
    broadcast_in_dim x2, local copies, waits for them, and re-layouts, gather_by_all_to_all(): jnp.broadcast_to(x[None], (n,) + x.shape)  1.38 us
    convert_element_type x1, other arithmetic, attention(): live.astype(jnp.int32).reshape(requests, 1, tok)  1.33 us
  transfers between devices with their start and end apart: 1, of which 1 were waited for; matrix products, arithmetic and copies ran while one was open for 4% of the time, Pallas kernels for 0%

profile of v3, /device:TPU:1, one launch (start us, length us, event | category | flops | bytes accessed | tf_op | source)
XLA Modules:
  0.0 63.4 jit_solution(7268774391575569994)
XLA Ops:
  0.6 0.0 copy-start
  0.6 1.4 %broadcast_in_dim.56 = bf16[16,2,512]{2,1,0:T(2,128)(2,1)} broadcast(bf16[2,512]{1,0:T(2,128)(2,1)} %param.6), dimensions={1,2} | broadcast | bytes 34816 | tf_op jit(solution)/shard_map/broadcast_in_dim | solution.py:18
  2.0 7.6 %all-to-all-start = ((bf16[16,2,512]{2,1,0:T(2,128)(2,1)}), bf16[16,2,512]{2,1,0:T(2,128)(2,1)S(1)}, u32[]{:S(2)}, u32[]{:S(2)}) async-start(bf16[16,2,512]{2,1,0:T(2,128)(2,1)} %broadcast_in_dim.56), calls=%async_computation | async-start | bytes 65536 | tf_op jit(solution)/shard_map/all_to_all | solution.py:18
  9.6 0.9 %compare_reduce_fusion = pred[2,16]{1,0:T(4,128)(4,1)S(1)} fusion(s32[2,32]{1,0:T(2,128)} %param.9, s32[16]{0:T(128)S(1)} %iota_add_fusion.1), kind=kLoop, calls=%fused_computation.11 | loop fusion | flops 2016 | bytes 352 | tf_op jit(solution)/shard_map/reduce_or | solution.py:85
  10.5 0.1 broadcast_in_dim.61
  10.6 0.1 reshape.137
  10.6 1.3 %and_convert_fusion.live_ref = s32[2,1,1024]{2,1,0:T(1,128)} fusion(pred[2,1,1024]{2,1,0:T(4,128)(4,1)S(1)} %reshape.137, s32[1024]{0:T(1024)S(1)} %iota_add_fusion, s32[2]{0:T(128)} %param.10), kind=kLoop, calls=%fused_computation.10 | loop fusion | flops 6144 | bytes 14344 | tf_op jit(solution)/shard_map/convert_element_type | solution.py:66
  12.0 0.1 iota_compare_fusion
  12.1 0.1 broadcast_in_dim.53
  12.2 3.8 %all-to-all-done = bf16[16,2,512]{2,1,0:T(2,128)(2,1)S(1)} async-done(((bf16[16,2,512]{2,1,0:T(2,128)(2,1)}), bf16[16,2,512]{2,1,0:T(2,128)(2,1)S(1)}, u32[]{:S(2)}, u32[]{:S(2)}) %all-to-all-start) | async-done | bytes 32800 | tf_op jit(solution)/shard_map/all_to_all | solution.py:18
  16.1 0.1 broadcast_in_dim.59
  16.3 0.7 %broadcast_select_fusion.q_ref = bf16[2,64,1024]{2,1,0:T(8,128)(2,1)} fusion(bf16[2,64,1024]{2,1,0:T(8,128)(2,1)S(1)} %broadcast_in_dim.59, pred[64,1024]{1,0:T(8,128)(4,1)S(1)} %bitcast.32), kind=kLoop, calls=%fused_computation.3 | loop fusion | flops 131072 | bytes 589824 | tf_op jit(solution)/shard_map/jit(_where)/select_n | solution.py:91
  17.0 5.5 %shard_map.77 = (f32[2,64,128]{2,1,0:T(8,128)}, f32[2,64,128]{2,1,0:T(8,128)}) custom-call(bf16[2,64,1024]{2,1,0:T(8,128)(2,1)} %broadcast_select_fusion.q_ref, s32[2,1,1024]{2,1,0:T(1,128)} %and_convert_fusion.live_ref, bf16[2,1024,1024]{2,1,0:T(8,128)(2,1)} %k_ref.1, bf16[2,1024,1024]{2,1,0:T(8,128)(2,1)} %v_ref.1), custom_call_target="tpu_custom_call" | custom-call | flops 536870912 | bytes 8650752 | tf_op jit(solution)/shard_map/pallas_call | solution.py:46
  22.5 0.9 %pad_maximum_fusion = f32[2,64,130]{2,1,0:T(8,128)S(1)} fusion(f32[2,64,2]{2,1,0:T(8,128)} %bitcast.35, f32[2,64,128]{2,1,0:T(8,128)} %get-tuple-element.4), kind=kLoop, calls=%fused_computation.4 | loop fusion | flops 16640 | bytes 133120 | tf_op jit(solution)/shard_map/concatenate | solution.py:97
  23.5 9.9 %all_to_all.20 = f32[16,2,4,130]{3,2,1,0:T(4,128)S(1)} all-to-all(f32[16,2,4,130]{3,2,1,0:T(4,128)S(1)} %bitcast.31), channel_id=1, replica_groups=mesh['grp'=16,'seq'=16] {'seq'}, dimensions={0} | all-to-all | bytes 133120 | tf_op jit(solution)/shard_map/all_to_all | solution.py:108
  33.4 0.1 fusion.8
  33.5 0.1 copy.54
  33.6 0.1 exponential_bitcast_fusion
  33.7 0.1 copy.47
  33.8 0.1 copy.49
  33.9 0.2 fusion.6
  34.1 0.1 fusion.2
  34.2 0.1 fusion.7
  34.3 0.0 copy-start.1
  34.3 18.9 %all_to_all.21 = bf16[16,2,512]{2,1,0:T(2,128)(2,1)S(1)} all-to-all(bf16[16,2,512]{2,1,0:T(2,128)(2,1)S(1)} %broadcast_in_dim.62), channel_id=1, replica_groups=mesh['grp'=16,'seq'=16] {'grp'}, dimensions={0} | all-to-all | bytes 65536 | tf_op jit(solution)/shard_map/all_to_all | solution.py:18
  53.2 0.0 copy-done
  53.2 0.2 fusion
  53.4 0.1 copy.52
  53.5 9.3 %all_to_all.22 = f32[16,2,512]{2,1,0:T(2,128)S(1)} all-to-all(f32[16,2,512]{2,1,0:T(2,128)S(1)} %copy.52), channel_id=1, replica_groups=mesh['grp'=16,'seq'=16] {'seq'}, dimensions={0} | all-to-all | bytes 131072 | tf_op jit(solution)/shard_map/all_to_all | solution.py:124
  62.8 0.6 reduce_sum.29
  63.4 0.0 copy-done.1
  (11 shorter events, 0.2 us)
Async XLA Ops:
  0.6 52.6 %copy-start = (bf16[512,512]{1,0:T(8,128)(2,1)S(1)}, bf16[512,512]{1,0:T(8,128)(2,1)}, u32[]{:S(2)}) copy-start(bf16[512,512]{1,0:T(8,128)(2,1)} %param.11) | copy-start | bytes 1572868
  2.0 14.1 %all-to-all-start = ((bf16[16,2,512]{2,1,0:T(2,128)(2,1)}), bf16[16,2,512]{2,1,0:T(2,128)(2,1)S(1)}, u32[]{:S(2)}, u32[]{:S(2)}) async-start(bf16[16,2,512]{2,1,0:T(2,128)(2,1)} %broadcast_in_dim.56), calls=%async_computation | async-start | bytes 65536 | tf_op jit(solution)/shard_map/all_to_all | solution.py:18
  34.3 29.1 %copy-start.1 = (bf16[1,2,4,128]{3,1,2,0:T(2,128)(2,1)}, bf16[1,2,4,128]{3,1,2,0:T(2,128)(2,1)S(1)}, u32[]{:S(2)}) copy-start(bf16[1,2,4,128]{3,1,2,0:T(2,128)(2,1)S(1)} %copy.65) | copy-start | bytes 6148

commit v4 on v3

v4 whole, which is shorter than its diff:
```python
import functools

import jax
import jax.numpy as jnp
from jax import lax
from jax.experimental import pallas as pl
from jax.experimental.pallas import tpu as pltpu
from jax.sharding import PartitionSpec as P

HEAD_DIMENSION = 128
PAGE = 64


NEG = -1e30


def gather_by_all_to_all(x, axis):
    n = lax.axis_size(axis)
    return lax.all_to_all(jnp.broadcast_to(x[None], (n,) + x.shape), axis, 0, 0, tiled=True)


def attention_kernel(h_ref, live_ref, k_ref, v_ref, out_ref, qd_ref, *, scale, head_group):
    _, nseq, local_width = h_ref.shape
    heads_dev = local_width // HEAD_DIMENSION
    q_heads = nseq * heads_dev
    qd_ref[...] = jnp.zeros(qd_ref.shape, qd_ref.dtype)
    for src in range(nseq):
        for i in range(heads_dev):
            h = src * heads_dev + i
            kv = h // head_group
            qd_ref[h:h + 1, kv * HEAD_DIMENSION:(kv + 1) * HEAD_DIMENSION] = h_ref[
                0, src:src + 1, i * HEAD_DIMENSION:(i + 1) * HEAD_DIMENSION
            ].astype(qd_ref.dtype)
    q = qd_ref[...].astype(jnp.bfloat16)
    live = live_ref[0] > 0
    scores = lax.dot_general(
        q, k_ref[0], (((1,), (1,)), ((), ())), preferred_element_type=jnp.float32
    ) * scale
    scores = jnp.where(live, scores, NEG)
    peak = jnp.max(scores, axis=-1, keepdims=True)
    weights = jnp.where(live, jnp.exp(scores - peak), 0.0)
    total = jnp.sum(weights, axis=-1, keepdims=True)
    full = jnp.dot(weights.astype(jnp.bfloat16), v_ref[0], preferred_element_type=jnp.float32)
    lane = lax.broadcasted_iota(jnp.int32, (q_heads, HEAD_DIMENSION), 1)
    stat = jnp.where(lane == 0, peak, jnp.where(lane == 1, total, 0.0))
    for d in range(nseq):
        rows = slice(d * heads_dev, (d + 1) * heads_dev)
        kv = d * heads_dev // head_group
        out_ref[d, 0, :, 0:HEAD_DIMENSION] = full[rows, kv * HEAD_DIMENSION:(kv + 1) * HEAD_DIMENSION]
        out_ref[d, 0, :, HEAD_DIMENSION:] = stat[rows, :]


def attention(heads_all, live, key_cache, value_store_cache, scale, head_group):
    nseq, requests, local_width = heads_all.shape
    heads_dev = local_width // HEAD_DIMENSION
    q_heads = nseq * heads_dev
    tok, width = key_cache.shape[1:]
    kernel = functools.partial(attention_kernel, scale=scale, head_group=head_group)
    flops = 4 * requests * q_heads * tok * width
    nbytes = 2 * (key_cache.size + value_store_cache.size + heads_all.size)
    return pl.pallas_call(
        kernel,
        grid=(requests,),
        in_specs=[
            pl.BlockSpec((1, nseq, local_width), lambda r: (r, 0, 0)),
            pl.BlockSpec((1, 1, tok), lambda r: (r, 0, 0)),
            pl.BlockSpec((1, tok, width), lambda r: (r, 0, 0)),
            pl.BlockSpec((1, tok, width), lambda r: (r, 0, 0)),
        ],
        out_specs=pl.BlockSpec((nseq, 1, heads_dev, 2 * HEAD_DIMENSION), lambda r: (0, r, 0, 0)),
        out_shape=jax.ShapeDtypeStruct((nseq, requests, heads_dev, 2 * HEAD_DIMENSION), jnp.float32),
        scratch_shapes=[pltpu.VMEM((q_heads, width), jnp.float32)],
        cost_estimate=pl.CostEstimate(
            flops=flops, transcendentals=requests * q_heads * tok, bytes_accessed=nbytes
        ),
    )(jnp.transpose(heads_all, (1, 0, 2)), live.astype(jnp.int32).reshape(requests, 1, tok), key_cache, value_store_cache)


def body(query, key_cache, value_store_cache, selected, lengths, w_out):
    nseq = lax.axis_size("seq")
    me = lax.axis_index("seq")
    requests = query.shape[0]
    tok_local = key_cache.shape[1]
    kv_heads = key_cache.shape[2] // HEAD_DIMENSION
    heads_dev = query.shape[1] // HEAD_DIMENSION
    q_heads = heads_dev * nseq
    head_group = q_heads // kv_heads
    scale = HEAD_DIMENSION ** (-0.5)

    heads_all = gather_by_all_to_all(query, "seq")

    pages_local = tok_local // PAGE
    first_page = me * pages_local
    page_ids = first_page + jnp.arange(pages_local, dtype=jnp.int32)
    page_picked = jnp.any(selected[:, :, None] == page_ids[None, None, :], axis=1)
    positions = me * tok_local + jnp.arange(tok_local, dtype=jnp.int32)
    live = jnp.repeat(page_picked, PAGE, axis=1) & (positions[None, :] < lengths[:, None])

    packed = attention(heads_all, live, key_cache, value_store_cache, scale, head_group)
    parts = lax.all_to_all(packed, "seq", 0, 0, tiled=True)
    b_out = parts[..., :HEAD_DIMENSION]
    b_max = parts[..., HEAD_DIMENSION]
    b_sum = parts[..., HEAD_DIMENSION + 1]
    top = jnp.max(b_max, axis=0)
    factor = jnp.exp(b_max - top[None])
    whole_total = jnp.sum(b_sum * factor, axis=0)
    whole_accum = jnp.sum(b_out * factor[..., None], axis=0)
    attended = (
        (whole_accum / whole_total[..., None])
        .reshape(requests, heads_dev * HEAD_DIMENSION)
        .astype(jnp.bfloat16)
    )
    everyone = gather_by_all_to_all(attended, "grp").reshape(-1, attended.shape[1])
    partial = jnp.dot(everyone, w_out, preferred_element_type=jnp.float32)
    partial = partial.reshape(nseq, -1, partial.shape[1])
    pieces = lax.all_to_all(partial, "seq", 0, 0, tiled=True)
    projected = jnp.sum(pieces, axis=0).astype(jnp.bfloat16)
    return (attended, projected)


def solution(mesh):
    return jax.shard_map(
        body,
        mesh=mesh,
        in_specs=(
            P("grp", "seq"),
            P("grp", "seq", None),
            P("grp", "seq", None),
            P("grp", None),
            P("grp"),
            P("seq", "grp"),
        ),
        out_specs=(P("grp", "seq"), P("seq", "grp")),
        check_vma=False,
    )
```

time: 63.8 us -> 63 us (0.987)
  other arithmetic: 5.04 us -> 3.38 us
    concatenate x1 -> x0, other arithmetic: 0.88 us -> none  [body(): jnp.concatenate([accum.reshape(requests, q_heads, HEAD_DIMENSION), peak.r...]
    select_n x2 -> x0, other arithmetic: 0.72 us -> none  [the longest x1 0.72 us: body(): jnp.where(own_kv[None, :, :, None], qfull, jnp.zeros((), qfull.dtype))]
where the time goes in v4:
time: 63 us; the launch traced here: 62.6 us
  blocking collectives  38.5 us (61%)
  starting transfers between devices  7.57 us (12%)
  Pallas kernels  5.48 us (9%)
  waiting for transfers between devices  4.08 us (6%)
  other arithmetic  3.38 us (5%)
  local copies, waits for them, and re-layouts  2.71 us (4%)
  between operations  0.72 us (1%)
    all_to_all x1, blocking collectives, gather_by_all_to_all(): lax.all_to_all(jnp.broadcast_to(x[None], (n,) + x.shape), axis, 0, 0, til...  18.9 us
    all_to_all x1, blocking collectives, body(): parts = lax.all_to_all(packed, 'seq', 0, 0, tiled=True)  10.3 us
    all_to_all x1, blocking collectives, body(): pieces = lax.all_to_all(partial, 'seq', 0, 0, tiled=True)  9.32 us
    all_to_all x1, starting transfers between devices, gather_by_all_to_all(): lax.all_to_all(jnp.broadcast_to(x[None], (n,) + x.shape), axis, 0, 0, til...  7.57 us
    pallas_call x1, Pallas kernels, attention(): pl.pallas_call(kernel, grid=(requests,), in_specs=[pl.BlockSpec((1, nseq,...  5.48 us
    all_to_all x1, waiting for transfers between devices, gather_by_all_to_all(): lax.all_to_all(jnp.broadcast_to(x[None], (n,) + x.shape), axis, 0, 0, til...  4.08 us
    broadcast_in_dim x2, local copies, waits for them, and re-layouts, gather_by_all_to_all(): jnp.broadcast_to(x[None], (n,) + x.shape)  1.38 us
    convert_element_type x1, other arithmetic, attention(): live.astype(jnp.int32).reshape(requests, 1, tok)  1.33 us
  transfers between devices with their start and end apart: 1, of which 1 were waited for; matrix products, arithmetic and copies ran while one was open for 4% of the time, Pallas kernels for 0%

profile of v4, /device:TPU:1, one launch (start us, length us, event | category | flops | bytes accessed | tf_op | source)
XLA Modules:
  0.0 62.6 jit_solution(17825292501809504334)
XLA Ops:
  0.6 0.0 copy-start
  0.6 1.4 %broadcast_in_dim.6 = bf16[16,2,512]{2,1,0:T(2,128)(2,1)} broadcast(bf16[2,512]{1,0:T(2,128)(2,1)} %param.6), dimensions={1,2} | broadcast | bytes 34816 | tf_op jit(solution)/shard_map/broadcast_in_dim | solution.py:19
  2.0 7.6 %all-to-all-start = ((bf16[16,2,512]{2,1,0:T(2,128)(2,1)}), bf16[16,2,512]{2,1,0:T(2,128)(2,1)S(1)}, u32[]{:S(2)}, u32[]{:S(2)}) async-start(bf16[16,2,512]{2,1,0:T(2,128)(2,1)} %broadcast_in_dim.6), calls=%async_computation | async-start | bytes 65536 | tf_op jit(solution)/shard_map/all_to_all | solution.py:19
  9.6 0.9 %compare_reduce_fusion = pred[2,16]{1,0:T(4,128)(4,1)S(1)} fusion(s32[2,32]{1,0:T(2,128)} %param.9, s32[16]{0:T(128)S(1)} %iota_add_fusion.1), kind=kLoop, calls=%fused_computation.8 | loop fusion | flops 2016 | bytes 352 | tf_op jit(solution)/shard_map/reduce_or | solution.py:95
  10.5 0.1 broadcast_in_dim.7
  10.6 0.1 reshape.93
  10.6 1.3 %and_convert_fusion.live_ref = s32[2,1,1024]{2,1,0:T(1,128)} fusion(pred[2,1,1024]{2,1,0:T(4,128)(4,1)S(1)} %reshape.93, s32[1024]{0:T(1024)S(1)} %iota_add_fusion, s32[2]{0:T(128)} %param.10), kind=kLoop, calls=%fused_computation.7 | loop fusion | flops 6144 | bytes 14344 | tf_op jit(solution)/shard_map/convert_element_type | solution.py:76
  12.0 4.1 %all-to-all-done = bf16[16,2,512]{2,1,0:T(2,128)(2,1)S(1)} async-done(((bf16[16,2,512]{2,1,0:T(2,128)(2,1)}), bf16[16,2,512]{2,1,0:T(2,128)(2,1)S(1)}, u32[]{:S(2)}, u32[]{:S(2)}) %all-to-all-start) | async-done | bytes 32800 | tf_op jit(solution)/shard_map/all_to_all | solution.py:19
  16.1 0.6 copy.47
  16.7 5.5 %shard_map.77 = f32[16,2,4,256]{3,2,1,0:T(4,128)} custom-call(bf16[2,16,512]{2,1,0:T(8,128)(2,1)} %bitcast.22, s32[2,1,1024]{2,1,0:T(1,128)} %and_convert_fusion.live_ref, bf16[2,1024,1024]{2,1,0:T(8,128)(2,1)} %k_ref.1, bf16[2,1024,1024]{2,1,0:T(8,128)(2,1)} %v_ref.1), custom_call_target="tpu_custom_call" | custom-call | flops 536870912 | bytes 8421376 | tf_op jit(solution)/shard_map/pallas_call | solution.py:61
  22.1 10.3 %all_to_all.20 = f32[16,2,4,256]{3,2,1,0:T(4,128)S(1)} all-to-all(f32[16,2,4,256]{3,2,1,0:T(4,128)} %shard_map.77), channel_id=1, replica_groups=mesh['grp'=16,'seq'=16] {'seq'}, dimensions={0} | all-to-all | bytes 262144 | tf_op jit(solution)/shard_map/all_to_all | solution.py:100
  32.4 0.1 fusion.8
  32.6 0.1 copy.38
  32.7 0.1 copy.39
  32.8 0.1 subtract_exponential_fusion
  32.9 0.1 copy.36
  33.1 0.1 copy.37
  33.2 0.2 fusion.6
  33.3 0.1 fusion.2
  33.4 0.1 fusion.7
  33.5 0.0 copy-start.1
  33.6 18.9 %all_to_all.21 = bf16[16,2,512]{2,1,0:T(2,128)(2,1)S(1)} all-to-all(bf16[16,2,512]{2,1,0:T(2,128)(2,1)S(1)} %broadcast_in_dim.8), channel_id=1, replica_groups=mesh['grp'=16,'seq'=16] {'grp'}, dimensions={0} | all-to-all | bytes 65536 | tf_op jit(solution)/shard_map/all_to_all | solution.py:19
  52.5 0.0 copy-done
  52.5 0.2 fusion
  52.6 0.1 copy.41
  52.7 9.3 %all_to_all.22 = f32[16,2,512]{2,1,0:T(2,128)S(1)} all-to-all(f32[16,2,512]{2,1,0:T(2,128)S(1)} %copy.41), channel_id=1, replica_groups=mesh['grp'=16,'seq'=16] {'seq'}, dimensions={0} | all-to-all | bytes 131072 | tf_op jit(solution)/shard_map/all_to_all | solution.py:116
  62.0 0.6 reduce_sum.29
  62.6 0.0 copy-done.1
  (4 shorter events, 0.0 us)
Async XLA Ops:
  0.6 51.8 %copy-start = (bf16[512,512]{1,0:T(8,128)(2,1)S(1)}, bf16[512,512]{1,0:T(8,128)(2,1)}, u32[]{:S(2)}) copy-start(bf16[512,512]{1,0:T(8,128)(2,1)} %param.11) | copy-start | bytes 1572868
  2.0 14.1 %all-to-all-start = ((bf16[16,2,512]{2,1,0:T(2,128)(2,1)}), bf16[16,2,512]{2,1,0:T(2,128)(2,1)S(1)}, u32[]{:S(2)}, u32[]{:S(2)}) async-start(bf16[16,2,512]{2,1,0:T(2,128)(2,1)} %broadcast_in_dim.6), calls=%async_computation | async-start | bytes 65536 | tf_op jit(solution)/shard_map/all_to_all | solution.py:19
  33.5 29.1 %copy-start.1 = (bf16[1,2,4,128]{3,1,2,0:T(2,128)(2,1)}, bf16[1,2,4,128]{3,1,2,0:T(2,128)(2,1)S(1)}, u32[]{:S(2)}) copy-start(bf16[1,2,4,128]{3,1,2,0:T(2,128)(2,1)S(1)} %copy.48) | copy-start | bytes 6148

commit v5 on v4

--- a/solution.py
+++ b/solution.py
@@ -20,18 +20,23 @@
 
 
 def attention_kernel(h_ref, live_ref, k_ref, v_ref, out_ref, qd_ref, *, scale, head_group):
-    _, nseq, local_width = h_ref.shape
+    nseq, requests, local_width = h_ref.shape
     heads_dev = local_width // HEAD_DIMENSION
     q_heads = nseq * heads_dev
-    qd_ref[...] = jnp.zeros(qd_ref.shape, qd_ref.dtype)
-    for src in range(nseq):
-        for i in range(heads_dev):
-            h = src * heads_dev + i
-            kv = h // head_group
-            qd_ref[h:h + 1, kv * HEAD_DIMENSION:(kv + 1) * HEAD_DIMENSION] = h_ref[
-                0, src:src + 1, i * HEAD_DIMENSION:(i + 1) * HEAD_DIMENSION
-            ].astype(qd_ref.dtype)
-    q = qd_ref[...].astype(jnp.bfloat16)
+
+    @pl.when(pl.program_id(0) == 0)
+    def _():
+        qd_ref[...] = jnp.zeros(qd_ref.shape, qd_ref.dtype)
+        for r in range(requests):
+            for src in range(nseq):
+                for i in range(heads_dev):
+                    h = src * heads_dev + i
+                    kv = h // head_group
+                    qd_ref[r, h:h + 1, kv * HEAD_DIMENSION:(kv + 1) * HEAD_DIMENSION] = h_ref[
+                        src, r:r + 1, i * HEAD_DIMENSION:(i + 1) * HEAD_DIMENSION
+                    ].astype(qd_ref.dtype)
+
+    q = qd_ref[pl.program_id(0)].astype(jnp.bfloat16)
     live = live_ref[0] > 0
     scores = lax.dot_general(
         q, k_ref[0], (((1,), (1,)), ((), ())), preferred_element_type=jnp.float32
@@ -62,18 +67,52 @@
         kernel,
         grid=(requests,),
         in_specs=[
-            pl.BlockSpec((1, nseq, local_width), lambda r: (r, 0, 0)),
+            pl.BlockSpec((nseq, requests, local_width), lambda r: (0, 0, 0)),
             pl.BlockSpec((1, 1, tok), lambda r: (r, 0, 0)),
             pl.BlockSpec((1, tok, width), lambda r: (r, 0, 0)),
             pl.BlockSpec((1, tok, width), lambda r: (r, 0, 0)),
         ],
         out_specs=pl.BlockSpec((nseq, 1, heads_dev, 2 * HEAD_DIMENSION), lambda r: (0, r, 0, 0)),
         out_shape=jax.ShapeDtypeStruct((nseq, requests, heads_dev, 2 * HEAD_DIMENSION), jnp.float32),
-        scratch_shapes=[pltpu.VMEM((q_heads, width), jnp.float32)],
+        scratch_shapes=[pltpu.VMEM((requests, q_heads, width), jnp.float32)],
         cost_estimate=pl.CostEstimate(
             flops=flops, transcendentals=requests * q_heads * tok, bytes_accessed=nbytes
         ),
-    )(jnp.transpose(heads_all, (1, 0, 2)), live.astype(jnp.int32).reshape(requests, 1, tok), key_cache, value_store_cache)
+    )(heads_all, live.astype(jnp.int32).reshape(requests, 1, tok), key_cache, value_store_cache)
+
+
+def combine_kernel(p_ref, att_ref, bcast_ref):
+    nseq, requests, heads_dev, _ = p_ref.shape
+    rows = []
+    for r in range(requests):
+        part = p_ref[:, r]
+        b_out = part[:, :, :HEAD_DIMENSION]
+        b_max = part[:, :, HEAD_DIMENSION:HEAD_DIMENSION + 1]
+        b_sum = part[:, :, HEAD_DIMENSION + 1:HEAD_DIMENSION + 2]
+        top = jnp.max(b_max, axis=0)
+        factor = jnp.exp(b_max - top[None])
+        whole_total = jnp.sum(b_sum * factor, axis=0)
+        whole_accum = jnp.sum(b_out * factor, axis=0)
+        merged = whole_accum / whole_total
+        rows.append(jnp.concatenate([merged[i:i + 1] for i in range(heads_dev)], axis=1))
+    attended = jnp.concatenate(rows, axis=0).astype(att_ref.dtype)
+    att_ref[...] = attended
+    bcast_ref[...] = jnp.broadcast_to(attended[None], bcast_ref.shape)
+
+
+def combine(parts, bcast_count):
+    nseq, requests, heads_dev, _ = parts.shape
+    vmem = pl.BlockSpec(memory_space=pltpu.VMEM)
+    width = heads_dev * HEAD_DIMENSION
+    return pl.pallas_call(
+        combine_kernel,
+        in_specs=[vmem],
+        out_specs=[vmem, vmem],
+        out_shape=[
+            jax.ShapeDtypeStruct((requests, width), jnp.bfloat16),
+            jax.ShapeDtypeStruct((bcast_count, requests, width), jnp.bfloat16),
+        ],
+    )(parts)
 
 
 def body(query, key_cache, value_store_cache, selected, lengths, w_out):
@@ -98,19 +137,8 @@
 
     packed = attention(heads_all, live, key_cache, value_store_cache, scale, head_group)
     parts = lax.all_to_all(packed, "seq", 0, 0, tiled=True)
-    b_out = parts[..., :HEAD_DIMENSION]
-    b_max = parts[..., HEAD_DIMENSION]
-    b_sum = parts[..., HEAD_DIMENSION + 1]
-    top = jnp.max(b_max, axis=0)
-    factor = jnp.exp(b_max - top[None])
-    whole_total = jnp.sum(b_sum * factor, axis=0)
-    whole_accum = jnp.sum(b_out * factor[..., None], axis=0)
-    attended = (
-        (whole_accum / whole_total[..., None])
-        .reshape(requests, heads_dev * HEAD_DIMENSION)
-        .astype(jnp.bfloat16)
-    )
-    everyone = gather_by_all_to_all(attended, "grp").reshape(-1, attended.shape[1])
+    attended, spread = combine(parts, lax.axis_size("grp"))
+    everyone = lax.all_to_all(spread, "grp", 0, 0, tiled=True).reshape(-1, attended.shape[1])
     partial = jnp.dot(everyone, w_out, preferred_element_type=jnp.float32)
     partial = partial.reshape(nseq, -1, partial.shape[1])
     pieces = lax.all_to_all(partial, "seq", 0, 0, tiled=True)

time: 63 us -> 65 us (1.032)
  Pallas kernels: 5.48 us -> 7.65 us
  blocking collectives: 38.5 us -> 39.4 us
    pallas_call x1 -> x2, Pallas kernels: 5.48 us -> 7.65 us  [the longest x1 5.95 us: attention(): pl.pallas_call(kernel, grid=(requests,), in_specs=[pl.BlockSpec((nseq, re...]
    all_to_all x1, blocking collectives: 10.3 us -> 11 us  [body(): parts = lax.all_to_all(packed, 'seq', 0, 0, tiled=True)]
    broadcast_in_dim x2 -> x1, local copies, waits for them, and re-layouts: 1.38 us -> 1.36 us  [gather_by_all_to_all(): jnp.broadcast_to(x[None], (n,) + x.shape)]
where the time goes in v5:
time: 65 us; the launch traced here: 64.6 us
  blocking collectives  39.4 us (61%)
  Pallas kernels  7.65 us (12%)
  starting transfers between devices  7.57 us (12%)
  waiting for transfers between devices  4.08 us (6%)
  other arithmetic  2.82 us (4%)
  local copies, waits for them, and re-layouts  2.2 us (3%)
  between operations  0.68 us (1%)
    all_to_all x1, blocking collectives, body(): lax.all_to_all(spread, 'grp', 0, 0, tiled=True)  19.1 us
    all_to_all x1, blocking collectives, body(): parts = lax.all_to_all(packed, 'seq', 0, 0, tiled=True)  11 us
    all_to_all x1, blocking collectives, body(): pieces = lax.all_to_all(partial, 'seq', 0, 0, tiled=True)  9.32 us
    all_to_all x1, starting transfers between devices, gather_by_all_to_all(): lax.all_to_all(jnp.broadcast_to(x[None], (n,) + x.shape), axis, 0, 0, til...  7.57 us
    pallas_call x1, Pallas kernels, attention(): pl.pallas_call(kernel, grid=(requests,), in_specs=[pl.BlockSpec((nseq, re...  5.95 us
    all_to_all x1, waiting for transfers between devices, gather_by_all_to_all(): lax.all_to_all(jnp.broadcast_to(x[None], (n,) + x.shape), axis, 0, 0, til...  4.08 us
    pallas_call x1, Pallas kernels, combine(): pl.pallas_call(combine_kernel, in_specs=[vmem], out_specs=[vmem, vmem], o...  1.7 us
    broadcast_in_dim x1, local copies, waits for them, and re-layouts, gather_by_all_to_all(): jnp.broadcast_to(x[None], (n,) + x.shape)  1.36 us
  transfers between devices with their start and end apart: 1, of which 1 were waited for; matrix products, arithmetic and copies ran while one was open for 4% of the time, Pallas kernels for 0%

profile of v5, /device:TPU:1, one launch (start us, length us, event | category | flops | bytes accessed | tf_op | source)
XLA Modules:
  0.0 64.6 jit_solution(17500476554474025302)
XLA Ops:
  0.6 0.0 copy-start
  0.6 1.4 %broadcast_in_dim.4 = bf16[16,2,512]{2,1,0:T(2,128)(2,1)} broadcast(bf16[2,512]{1,0:T(2,128)(2,1)} %param.6), dimensions={1,2} | broadcast | bytes 34816 | tf_op jit(solution)/shard_map/broadcast_in_dim | solution.py:19
  2.0 7.6 %all-to-all-start = ((bf16[16,2,512]{2,1,0:T(2,128)(2,1)}), bf16[16,2,512]{2,1,0:T(2,128)(2,1)S(1)}, u32[]{:S(2)}, u32[]{:S(2)}) async-start(bf16[16,2,512]{2,1,0:T(2,128)(2,1)} %broadcast_in_dim.4), calls=%async_computation | async-start | bytes 65536 | tf_op jit(solution)/shard_map/all_to_all | solution.py:19
  9.6 0.9 %compare_reduce_fusion = pred[2,16]{1,0:T(4,128)(4,1)S(1)} fusion(s32[2,32]{1,0:T(2,128)} %param.9, s32[16]{0:T(128)S(1)} %iota_add_fusion.1), kind=kLoop, calls=%fused_computation.4 | loop fusion | flops 2016 | bytes 352 | tf_op jit(solution)/shard_map/reduce_or | solution.py:134
  10.5 0.1 broadcast_in_dim.5
  10.6 0.1 reshape.76
  10.6 1.3 %and_convert_fusion.live_ref = s32[2,1,1024]{2,1,0:T(1,128)} fusion(pred[2,1,1024]{2,1,0:T(4,128)(4,1)S(1)} %reshape.76, s32[1024]{0:T(1024)S(1)} %iota_add_fusion, s32[2]{0:T(128)} %param.10), kind=kLoop, calls=%fused_computation.3 | loop fusion | flops 6144 | bytes 14344 | tf_op jit(solution)/shard_map/convert_element_type | solution.py:81
  12.0 4.1 %all-to-all-done.h_ref = bf16[16,2,512]{2,1,0:T(2,128)(2,1)S(1)} async-done(((bf16[16,2,512]{2,1,0:T(2,128)(2,1)}), bf16[16,2,512]{2,1,0:T(2,128)(2,1)S(1)}, u32[]{:S(2)}, u32[]{:S(2)}) %all-to-all-start) | async-done | bytes 32800 | tf_op jit(solution)/shard_map/all_to_all | solution.py:19
  16.1 0.0 copy-start.1
  16.1 0.6 copy-done.1
  16.7 6.0 %shard_map.77 = f32[16,2,4,256]{3,2,1,0:T(4,128)} custom-call(bf16[16,2,512]{2,1,0:T(2,128)(2,1)} %copy-done.1, s32[2,1,1024]{2,1,0:T(1,128)} %and_convert_fusion.live_ref, bf16[2,1024,1024]{2,1,0:T(8,128)(2,1)} %k_ref.1, bf16[2,1024,1024]{2,1,0:T(8,128)(2,1)} %v_ref.1), custom_call_target="tpu_custom_call" | custom-call | flops 536870912 | bytes 8421376 | tf_op jit(solution)/shard_map/pallas_call | solution.py:66
  22.6 11.0 %all_to_all.20.p_ref = f32[16,2,4,256]{3,2,1,0:T(4,128)} all-to-all(f32[16,2,4,256]{3,2,1,0:T(4,128)} %shard_map.77), channel_id=1, replica_groups=mesh['grp'=16,'seq'=16] {'seq'}, dimensions={0} | all-to-all | bytes 262144 | tf_op jit(solution)/shard_map/all_to_all | solution.py:139
  33.6 1.7 %shard_map.78 = (bf16[2,512]{1,0:T(2,128)(2,1)}, bf16[16,2,512]{2,1,0:T(2,128)(2,1)}) custom-call(f32[16,2,4,256]{3,2,1,0:T(4,128)} %all_to_all.20.p_ref), custom_call_target="tpu_custom_call" | custom-call | tf_op jit(solution)/shard_map/pallas_call | solution.py:107
  35.3 19.1 %all_to_all.21 = bf16[16,2,512]{2,1,0:T(2,128)(2,1)S(1)} all-to-all(bf16[16,2,512]{2,1,0:T(2,128)(2,1)} %get-tuple-element.5), channel_id=1, replica_groups=mesh['grp'=16,'seq'=16] {'grp'}, dimensions={0} | all-to-all | bytes 65536 | tf_op jit(solution)/shard_map/all_to_all | solution.py:141
  54.4 0.0 copy-done
  54.4 0.2 fusion
  54.6 0.1 copy.20
  54.7 9.3 %all_to_all.22 = f32[16,2,512]{2,1,0:T(2,128)S(1)} all-to-all(f32[16,2,512]{2,1,0:T(2,128)S(1)} %copy.20), channel_id=1, replica_groups=mesh['grp'=16,'seq'=16] {'seq'}, dimensions={0} | all-to-all | bytes 131072 | tf_op jit(solution)/shard_map/all_to_all | solution.py:144
  64.0 0.6 reduce_sum.9
  (2 shorter events, 0.0 us)
Async XLA Ops:
  0.6 53.8 %copy-start = (bf16[512,512]{1,0:T(8,128)(2,1)S(1)}, bf16[512,512]{1,0:T(8,128)(2,1)}, u32[]{:S(2)}) copy-start(bf16[512,512]{1,0:T(8,128)(2,1)} %param.11) | copy-start | bytes 1572868
  2.0 14.1 %all-to-all-start = ((bf16[16,2,512]{2,1,0:T(2,128)(2,1)}), bf16[16,2,512]{2,1,0:T(2,128)(2,1)S(1)}, u32[]{:S(2)}, u32[]{:S(2)}) async-start(bf16[16,2,512]{2,1,0:T(2,128)(2,1)} %broadcast_in_dim.4), calls=%async_computation | async-start | bytes 65536 | tf_op jit(solution)/shard_map/all_to_all | solution.py:19
  16.1 0.6 copy-start.1

commit v6 on v4

--- a/solution.py
+++ b/solution.py
@@ -19,7 +19,7 @@
     return lax.all_to_all(jnp.broadcast_to(x[None], (n,) + x.shape), axis, 0, 0, tiled=True)
 
 
-def attention_kernel(h_ref, live_ref, k_ref, v_ref, out_ref, qd_ref, *, scale, head_group):
+def attention_kernel(sel_ref, lim_ref, base_ref, h_ref, k_ref, v_ref, out_ref, qd_ref, *, scale, head_group):
     _, nseq, local_width = h_ref.shape
     heads_dev = local_width // HEAD_DIMENSION
     q_heads = nseq * heads_dev
@@ -32,7 +32,14 @@
                 0, src:src + 1, i * HEAD_DIMENSION:(i + 1) * HEAD_DIMENSION
             ].astype(qd_ref.dtype)
     q = qd_ref[...].astype(jnp.bfloat16)
-    live = live_ref[0] > 0
+    r = pl.program_id(0)
+    tok = k_ref.shape[1]
+    lane = lax.broadcasted_iota(jnp.int32, (1, tok), 1)
+    page = base_ref[0] + lane // PAGE
+    picked = page == sel_ref[r, 0]
+    for j in range(1, sel_ref.shape[1]):
+        picked = picked | (page == sel_ref[r, j])
+    live = picked & (lane < lim_ref[r])
     scores = lax.dot_general(
         q, k_ref[0], (((1,), (1,)), ((), ())), preferred_element_type=jnp.float32
     ) * scale
@@ -50,7 +57,7 @@
         out_ref[d, 0, :, HEAD_DIMENSION:] = stat[rows, :]
 
 
-def attention(heads_all, live, key_cache, value_store_cache, scale, head_group):
+def attention(heads_all, selected, limit, base, key_cache, value_store_cache, scale, head_group):
     nseq, requests, local_width = heads_all.shape
     heads_dev = local_width // HEAD_DIMENSION
     q_heads = nseq * heads_dev
@@ -62,8 +69,10 @@
         kernel,
         grid=(requests,),
         in_specs=[
+            pl.BlockSpec(memory_space=pltpu.SMEM),
+            pl.BlockSpec(memory_space=pltpu.SMEM),
+            pl.BlockSpec(memory_space=pltpu.SMEM),
             pl.BlockSpec((1, nseq, local_width), lambda r: (r, 0, 0)),
-            pl.BlockSpec((1, 1, tok), lambda r: (r, 0, 0)),
             pl.BlockSpec((1, tok, width), lambda r: (r, 0, 0)),
             pl.BlockSpec((1, tok, width), lambda r: (r, 0, 0)),
         ],
@@ -73,7 +82,7 @@
         cost_estimate=pl.CostEstimate(
             flops=flops, transcendentals=requests * q_heads * tok, bytes_accessed=nbytes
         ),
-    )(jnp.transpose(heads_all, (1, 0, 2)), live.astype(jnp.int32).reshape(requests, 1, tok), key_cache, value_store_cache)
+    )(selected, limit, base, jnp.transpose(heads_all, (1, 0, 2)), key_cache, value_store_cache)
 
 
 def body(query, key_cache, value_store_cache, selected, lengths, w_out):
@@ -89,14 +98,9 @@
 
     heads_all = gather_by_all_to_all(query, "seq")
 
-    pages_local = tok_local // PAGE
-    first_page = me * pages_local
-    page_ids = first_page + jnp.arange(pages_local, dtype=jnp.int32)
-    page_picked = jnp.any(selected[:, :, None] == page_ids[None, None, :], axis=1)
-    positions = me * tok_local + jnp.arange(tok_local, dtype=jnp.int32)
-    live = jnp.repeat(page_picked, PAGE, axis=1) & (positions[None, :] < lengths[:, None])
-
-    packed = attention(heads_all, live, key_cache, value_store_cache, scale, head_group)
+    limit = (lengths - me * tok_local).astype(jnp.int32)
+    base = jnp.reshape(me * (tok_local // PAGE), (1,)).astype(jnp.int32)
+    packed = attention(heads_all, selected, limit, base, key_cache, value_store_cache, scale, head_group)
     parts = lax.all_to_all(packed, "seq", 0, 0, tiled=True)
     b_out = parts[..., :HEAD_DIMENSION]
     b_max = parts[..., HEAD_DIMENSION]

time: 63 us -> 63 us (level)
  waiting for transfers between devices: 4.08 us -> 5.3 us
  other arithmetic: 3.38 us -> 2.35 us
    convert_element_type x1 -> x0, other arithmetic: 1.33 us -> none  [attention(): live.astype(jnp.int32).reshape(requests, 1, tok)]
    all_to_all x1, waiting for transfers between devices: 4.08 us -> 5.3 us  [gather_by_all_to_all(): lax.all_to_all(jnp.broadcast_to(x[None], (n,) + x.shape), axis, 0, 0, til...]
    sub x0 -> x1, other arithmetic: none -> 1.17 us  [body(): limit = (lengths - me * tok_local).astype(jnp.int32)]
    reduce_or x1 -> x0, other arithmetic: 0.86 us -> none  [body(): jnp.any(selected[:, :, None] == page_ids[None, None, :], axis=1)]
  transfers between devices with their start and end apart: 1 -> 1, of which waited for: 1 -> 1; matrix products, arithmetic and copies ran while one was open for 4% -> 2% of each run, Pallas kernels for 0% -> 0%
where the time goes in v6:
time: 63 us; the launch traced here: 62.7 us
  blocking collectives  38.5 us (61%)
  starting transfers between devices  7.57 us (12%)
  Pallas kernels  5.52 us (9%)
  waiting for transfers between devices  5.3 us (8%)
  local copies, waits for them, and re-layouts  2.55 us (4%)
  other arithmetic  2.35 us (4%)
  between operations  0.7 us (1%)
    all_to_all x1, blocking collectives, gather_by_all_to_all(): lax.all_to_all(jnp.broadcast_to(x[None], (n,) + x.shape), axis, 0, 0, til...  18.9 us
    all_to_all x1, blocking collectives, body(): parts = lax.all_to_all(packed, 'seq', 0, 0, tiled=True)  10.3 us
    all_to_all x1, blocking collectives, body(): pieces = lax.all_to_all(partial, 'seq', 0, 0, tiled=True)  9.32 us
    all_to_all x1, starting transfers between devices, gather_by_all_to_all(): lax.all_to_all(jnp.broadcast_to(x[None], (n,) + x.shape), axis, 0, 0, til...  7.57 us
    pallas_call x1, Pallas kernels, attention(): pl.pallas_call(kernel, grid=(requests,), in_specs=[pl.BlockSpec(memory_sp...  5.52 us
    all_to_all x1, waiting for transfers between devices, gather_by_all_to_all(): lax.all_to_all(jnp.broadcast_to(x[None], (n,) + x.shape), axis, 0, 0, til...  5.3 us
    broadcast_in_dim x2, local copies, waits for them, and re-layouts, gather_by_all_to_all(): jnp.broadcast_to(x[None], (n,) + x.shape)  1.38 us
  transfers between devices with their start and end apart: 1, of which 1 were waited for; matrix products, arithmetic and copies ran while one was open for 2% of the time, Pallas kernels for 0%

profile of v6, /device:TPU:1, one launch (start us, length us, event | category | flops | bytes accessed | tf_op | source)
XLA Modules:
  0.0 62.7 jit_solution(117775706525183188)
XLA Ops:
  0.6 0.0 copy-start
  0.6 1.4 %broadcast_in_dim.4 = bf16[16,2,512]{2,1,0:T(2,128)(2,1)} broadcast(bf16[2,512]{1,0:T(2,128)(2,1)} %param.6), dimensions={1,2} | broadcast | bytes 34816 | tf_op jit(solution)/shard_map/broadcast_in_dim | solution.py:19
  2.0 7.6 %all-to-all-start = ((bf16[16,2,512]{2,1,0:T(2,128)(2,1)}), bf16[16,2,512]{2,1,0:T(2,128)(2,1)S(1)}, u32[]{:S(2)}, u32[]{:S(2)}) async-start(bf16[16,2,512]{2,1,0:T(2,128)(2,1)} %broadcast_in_dim.4), calls=%async_computation | async-start | bytes 65536 | tf_op jit(solution)/shard_map/all_to_all | solution.py:19
  9.6 1.2 %broadcast_subtract_fusion.lim_ref = s32[2]{0:T(128)} fusion(s32[2]{0:T(128)} %param.10, s32[]{:T(128)S(6)} %mul.19), kind=kLoop, calls=%fused_computation.14 | loop fusion | flops 2 | bytes 20 | tf_op jit(solution)/shard_map/sub | solution.py:101
  10.8 5.3 %all-to-all-done = bf16[16,2,512]{2,1,0:T(2,128)(2,1)S(1)} async-done(((bf16[16,2,512]{2,1,0:T(2,128)(2,1)}), bf16[16,2,512]{2,1,0:T(2,128)(2,1)S(1)}, u32[]{:S(2)}, u32[]{:S(2)}) %all-to-all-start) | async-done | bytes 32800 | tf_op jit(solution)/shard_map/all_to_all | solution.py:19
  16.1 0.6 copy.31
  16.7 5.5 %shard_map.77 = f32[16,2,4,256]{3,2,1,0:T(4,128)} custom-call(s32[2,32]{1,0:T(2,128)} %sel_ref.1, s32[2]{0:T(128)} %broadcast_subtract_fusion.lim_ref, s32[1]{0:T(128)} %bitcast.base_ref, bf16[2,16,512]{2,1,0:T(8,128)(2,1)} %bitcast.23, bf16[2,1024,1024]{2,1,0:T(8,128)(2,1)} %k_ref.1, bf16[2,1024,1024]{2,1,0:T(8,128)(2,1)} %v_ref.1), custom_call_target="tpu_custom_call" | custom-call | flops 536870912 | bytes 8421376 | tf_op jit(solution)/shard_map/pallas_call | solution.py:68
  22.2 10.3 %all_to_all.20 = f32[16,2,4,256]{3,2,1,0:T(4,128)S(1)} all-to-all(f32[16,2,4,256]{3,2,1,0:T(4,128)} %shard_map.77), channel_id=1, replica_groups=mesh['grp'=16,'seq'=16] {'seq'}, dimensions={0} | all-to-all | bytes 262144 | tf_op jit(solution)/shard_map/all_to_all | solution.py:104
  32.5 0.1 fusion.8
  32.6 0.1 copy.22
  32.7 0.1 copy.23
  32.9 0.1 subtract_exponential_fusion
  33.0 0.1 copy.20
  33.1 0.1 copy.21
  33.2 0.2 fusion.6
  33.4 0.1 fusion.2
  33.5 0.1 fusion.7
  33.6 0.0 copy-start.1
  33.6 18.9 %all_to_all.21 = bf16[16,2,512]{2,1,0:T(2,128)(2,1)S(1)} all-to-all(bf16[16,2,512]{2,1,0:T(2,128)(2,1)S(1)} %broadcast_in_dim.5), channel_id=1, replica_groups=mesh['grp'=16,'seq'=16] {'grp'}, dimensions={0} | all-to-all | bytes 65536 | tf_op jit(solution)/shard_map/all_to_all | solution.py:19
  52.5 0.0 copy-done
  52.5 0.2 fusion
  52.7 0.1 copy.25
  52.7 9.3 %all_to_all.22 = f32[16,2,512]{2,1,0:T(2,128)S(1)} all-to-all(f32[16,2,512]{2,1,0:T(2,128)S(1)} %copy.25), channel_id=1, replica_groups=mesh['grp'=16,'seq'=16] {'seq'}, dimensions={0} | all-to-all | bytes 131072 | tf_op jit(solution)/shard_map/all_to_all | solution.py:120
  62.1 0.6 reduce_sum.29
  62.7 0.0 copy-done.1
  (2 shorter events, 0.0 us)
Async XLA Ops:
  0.6 51.9 %copy-start = (bf16[512,512]{1,0:T(8,128)(2,1)S(1)}, bf16[512,512]{1,0:T(8,128)(2,1)}, u32[]{:S(2)}) copy-start(bf16[512,512]{1,0:T(8,128)(2,1)} %param.11) | copy-start | bytes 1572868
  2.0 14.1 %all-to-all-start = ((bf16[16,2,512]{2,1,0:T(2,128)(2,1)}), bf16[16,2,512]{2,1,0:T(2,128)(2,1)S(1)}, u32[]{:S(2)}, u32[]{:S(2)}) async-start(bf16[16,2,512]{2,1,0:T(2,128)(2,1)} %broadcast_in_dim.4), calls=%async_computation | async-start | bytes 65536 | tf_op jit(solution)/shard_map/all_to_all | solution.py:19
  33.6 29.1 %copy-start.1 = (bf16[1,2,4,128]{3,1,2,0:T(2,128)(2,1)}, bf16[1,2,4,128]{3,1,2,0:T(2,128)(2,1)S(1)}, u32[]{:S(2)}) copy-start(bf16[1,2,4,128]{3,1,2,0:T(2,128)(2,1)S(1)} %copy.32) | copy-start | bytes 6148

commit v7 on v6

--- a/solution.py
+++ b/solution.py
@@ -48,17 +48,18 @@
     weights = jnp.where(live, jnp.exp(scores - peak), 0.0)
     total = jnp.sum(weights, axis=-1, keepdims=True)
     full = jnp.dot(weights.astype(jnp.bfloat16), v_ref[0], preferred_element_type=jnp.float32)
-    lane = lax.broadcasted_iota(jnp.int32, (q_heads, HEAD_DIMENSION), 1)
-    stat = jnp.where(lane == 0, peak, jnp.where(lane == 1, total, 0.0))
+    peak_lanes = jnp.broadcast_to(peak, (q_heads, HEAD_DIMENSION))
+    total_lanes = jnp.broadcast_to(total, (q_heads, HEAD_DIMENSION))
     for d in range(nseq):
         rows = slice(d * heads_dev, (d + 1) * heads_dev)
         kv = d * heads_dev // head_group
         out_ref[d, 0, :, 0:HEAD_DIMENSION] = full[rows, kv * HEAD_DIMENSION:(kv + 1) * HEAD_DIMENSION]
-        out_ref[d, 0, :, HEAD_DIMENSION:] = stat[rows, :]
+        out_ref[d, 0, :, HEAD_DIMENSION:2 * HEAD_DIMENSION] = peak_lanes[rows, :]
+        out_ref[d, 0, :, 2 * HEAD_DIMENSION:] = total_lanes[rows, :]
 
 
 def attention(heads_all, selected, limit, base, key_cache, value_store_cache, scale, head_group):
-    nseq, requests, local_width = heads_all.shape
+    requests, nseq, local_width = heads_all.shape
     heads_dev = local_width // HEAD_DIMENSION
     q_heads = nseq * heads_dev
     tok, width = key_cache.shape[1:]
@@ -76,13 +77,13 @@
             pl.BlockSpec((1, tok, width), lambda r: (r, 0, 0)),
             pl.BlockSpec((1, tok, width), lambda r: (r, 0, 0)),
         ],
-        out_specs=pl.BlockSpec((nseq, 1, heads_dev, 2 * HEAD_DIMENSION), lambda r: (0, r, 0, 0)),
-        out_shape=jax.ShapeDtypeStruct((nseq, requests, heads_dev, 2 * HEAD_DIMENSION), jnp.float32),
+        out_specs=pl.BlockSpec((nseq, 1, heads_dev, 3 * HEAD_DIMENSION), lambda r: (0, r, 0, 0)),
+        out_shape=jax.ShapeDtypeStruct((nseq, requests, heads_dev, 3 * HEAD_DIMENSION), jnp.float32),
         scratch_shapes=[pltpu.VMEM((q_heads, width), jnp.float32)],
         cost_estimate=pl.CostEstimate(
             flops=flops, transcendentals=requests * q_heads * tok, bytes_accessed=nbytes
         ),
-    )(selected, limit, base, jnp.transpose(heads_all, (1, 0, 2)), key_cache, value_store_cache)
+    )(selected, limit, base, heads_all, key_cache, value_store_cache)
 
 
 def body(query, key_cache, value_store_cache, selected, lengths, w_out):
@@ -96,21 +97,23 @@
     head_group = q_heads // kv_heads
     scale = HEAD_DIMENSION ** (-0.5)
 
-    heads_all = gather_by_all_to_all(query, "seq")
+    heads_all = lax.all_to_all(
+        jnp.broadcast_to(query[:, None, :], (requests, nseq, query.shape[1])), "seq", 1, 1, tiled=True
+    )
 
     limit = (lengths - me * tok_local).astype(jnp.int32)
     base = jnp.reshape(me * (tok_local // PAGE), (1,)).astype(jnp.int32)
     packed = attention(heads_all, selected, limit, base, key_cache, value_store_cache, scale, head_group)
     parts = lax.all_to_all(packed, "seq", 0, 0, tiled=True)
     b_out = parts[..., :HEAD_DIMENSION]
-    b_max = parts[..., HEAD_DIMENSION]
-    b_sum = parts[..., HEAD_DIMENSION + 1]
+    b_max = parts[..., HEAD_DIMENSION:2 * HEAD_DIMENSION]
+    b_sum = parts[..., 2 * HEAD_DIMENSION:]
     top = jnp.max(b_max, axis=0)
     factor = jnp.exp(b_max - top[None])
     whole_total = jnp.sum(b_sum * factor, axis=0)
-    whole_accum = jnp.sum(b_out * factor[..., None], axis=0)
+    whole_accum = jnp.sum(b_out * factor, axis=0)
     attended = (
-        (whole_accum / whole_total[..., None])
+        (whole_accum / whole_total)
         .reshape(requests, heads_dev * HEAD_DIMENSION)
         .astype(jnp.bfloat16)
     )

time: 63 us -> 62.4 us (level)
    broadcast_in_dim x0 -> x1, local copies, waits for them, and re-layouts: none -> 1.36 us  [body(): jnp.broadcast_to(query[:, None, :], (requests, nseq, query.shape[1]))]
    broadcast_in_dim x2 -> x1, local copies, waits for them, and re-layouts: 1.38 us -> 0.02 us  [gather_by_all_to_all(): jnp.broadcast_to(x[None], (n,) + x.shape)]
where the time goes in v7:
time: 62.4 us; the launch traced here: 62 us
  blocking collectives  38.8 us (62%)
  starting transfers between devices  7.57 us (12%)
  Pallas kernels  5.56 us (9%)
  waiting for transfers between devices  5.3 us (8%)
  local copies, waits for them, and re-layouts  2.07 us (3%)
  other arithmetic  1.88 us (3%)
  between operations  0.69 us (1%)
    all_to_all x1, blocking collectives, gather_by_all_to_all(): lax.all_to_all(jnp.broadcast_to(x[None], (n,) + x.shape), axis, 0, 0, til...  18.9 us
    all_to_all x1, blocking collectives, body(): parts = lax.all_to_all(packed, 'seq', 0, 0, tiled=True)  10.7 us
    all_to_all x1, blocking collectives, body(): pieces = lax.all_to_all(partial, 'seq', 0, 0, tiled=True)  9.23 us
    all_to_all x1, starting transfers between devices, body(): lax.all_to_all(jnp.broadcast_to(query[:, None, :], (requests, nseq, query...  7.57 us
    pallas_call x1, Pallas kernels, attention(): pl.pallas_call(kernel, grid=(requests,), in_specs=[pl.BlockSpec(memory_sp...  5.56 us
    all_to_all x1, waiting for transfers between devices, body(): lax.all_to_all(jnp.broadcast_to(query[:, None, :], (requests, nseq, query...  5.3 us
    broadcast_in_dim x1, local copies, waits for them, and re-layouts, body(): jnp.broadcast_to(query[:, None, :], (requests, nseq, query.shape[1]))  1.36 us
  transfers between devices with their start and end apart: 1, of which 1 were waited for; matrix products, arithmetic and copies ran while one was open for 2% of the time, Pallas kernels for 0%

profile of v7, /device:TPU:1, one launch (start us, length us, event | category | flops | bytes accessed | tf_op | source)
XLA Modules:
  0.0 62.0 jit_solution(14320890327025654626)
XLA Ops:
  0.6 0.0 copy-start
  0.6 1.4 %broadcast_in_dim.4 = bf16[2,16,512]{2,0,1:T(2,128)(2,1)} broadcast(bf16[2,512]{1,0:T(2,128)(2,1)} %param.6), dimensions={0,2} | broadcast | bytes 34816 | tf_op jit(solution)/shard_map/broadcast_in_dim | solution.py:101
  2.0 7.6 %all-to-all-start = ((bf16[2,16,512]{2,0,1:T(2,128)(2,1)}), bf16[2,16,512]{2,0,1:T(2,128)(2,1)S(1)}, u32[]{:S(2)}, u32[]{:S(2)}) async-start(bf16[2,16,512]{2,0,1:T(2,128)(2,1)} %broadcast_in_dim.4), calls=%async_computation | async-start | bytes 65536 | tf_op jit(solution)/shard_map/all_to_all | solution.py:100
  9.6 1.2 %broadcast_subtract_fusion.lim_ref = s32[2]{0:T(128)} fusion(s32[2]{0:T(128)} %param.10, s32[]{:T(128)S(6)} %mul.12), kind=kLoop, calls=%fused_computation.12 | loop fusion | flops 2 | bytes 20 | tf_op jit(solution)/shard_map/sub | solution.py:104
  10.8 5.3 %all-to-all-done = bf16[2,16,512]{2,0,1:T(2,128)(2,1)S(1)} async-done(((bf16[2,16,512]{2,0,1:T(2,128)(2,1)}), bf16[2,16,512]{2,0,1:T(2,128)(2,1)S(1)}, u32[]{:S(2)}, u32[]{:S(2)}) %all-to-all-start) | async-done | bytes 32800 | tf_op jit(solution)/shard_map/all_to_all | solution.py:100
  16.1 0.6 copy.8.h_ref
  16.7 5.6 %shard_map.77 = f32[16,2,4,384]{3,2,1,0:T(4,128)} custom-call(s32[2,32]{1,0:T(2,128)} %sel_ref.1, s32[2]{0:T(128)} %broadcast_subtract_fusion.lim_ref, s32[1]{0:T(128)} %bitcast.base_ref, bf16[2,16,512]{2,1,0:T(8,128)(2,1)} %copy.8.h_ref, bf16[2,1024,1024]{2,1,0:T(8,128)(2,1)} %k_ref.1, bf16[2,1024,1024]{2,1,0:T(8,128)(2,1)} %v_ref.1), custom_call_target="tpu_custom_call" | custom-call | flops 536870912 | bytes 8421376 | tf_op jit(solution)/shard_map/pallas_call | solution.py:69
  22.2 10.7 %all_to_all.20 = f32[16,2,4,384]{3,2,1,0:T(4,128)S(1)} all-to-all(f32[16,2,4,384]{3,2,1,0:T(4,128)} %shard_map.77), channel_id=1, replica_groups=mesh['grp'=16,'seq'=16] {'seq'}, dimensions={0} | all-to-all | bytes 393216 | tf_op jit(solution)/shard_map/all_to_all | solution.py:107
  32.9 0.1 fusion.2
  33.0 0.0 copy-start.1
  33.0 18.9 %all_to_all.21 = bf16[16,2,512]{2,1,0:T(2,128)(2,1)S(1)} all-to-all(bf16[16,2,512]{2,1,0:T(2,128)(2,1)S(1)} %broadcast_in_dim.5), channel_id=1, replica_groups=mesh['grp'=16,'seq'=16] {'grp'}, dimensions={0} | all-to-all | bytes 65536 | tf_op jit(solution)/shard_map/all_to_all | solution.py:19
  51.9 0.0 copy-done
  51.9 0.2 fusion
  52.1 0.1 copy.10
  52.2 9.2 %all_to_all.22 = f32[16,2,512]{2,1,0:T(2,128)S(1)} all-to-all(f32[16,2,512]{2,1,0:T(2,128)S(1)} %copy.10), channel_id=1, replica_groups=mesh['grp'=16,'seq'=16] {'seq'}, dimensions={0} | all-to-all | bytes 131072 | tf_op jit(solution)/shard_map/all_to_all | solution.py:123
  61.4 0.6 reduce_sum.29
  62.0 0.0 copy-done.1
  (4 shorter events, 0.1 us)
Async XLA Ops:
  0.6 51.3 %copy-start = (bf16[512,512]{1,0:T(8,128)(2,1)S(1)}, bf16[512,512]{1,0:T(8,128)(2,1)}, u32[]{:S(2)}) copy-start(bf16[512,512]{1,0:T(8,128)(2,1)} %param.11) | copy-start | bytes 1572868
  2.0 14.1 %all-to-all-start = ((bf16[2,16,512]{2,0,1:T(2,128)(2,1)}), bf16[2,16,512]{2,0,1:T(2,128)(2,1)S(1)}, u32[]{:S(2)}, u32[]{:S(2)}) async-start(bf16[2,16,512]{2,0,1:T(2,128)(2,1)} %broadcast_in_dim.4), calls=%async_computation | async-start | bytes 65536 | tf_op jit(solution)/shard_map/all_to_all | solution.py:100
  33.0 29.0 %copy-start.1 = (bf16[1,2,4,128]{3,1,2,0:T(2,128)(2,1)}, bf16[1,2,4,128]{3,1,2,0:T(2,128)(2,1)S(1)}, u32[]{:S(2)}) copy-start(bf16[1,2,4,128]{3,1,2,0:T(2,128)(2,1)S(1)} %copy.15) | copy-start | bytes 6148

commit v8 on v7

--- a/solution.py
+++ b/solution.py
@@ -119,9 +119,10 @@
     )
     everyone = gather_by_all_to_all(attended, "grp").reshape(-1, attended.shape[1])
     partial = jnp.dot(everyone, w_out, preferred_element_type=jnp.float32)
-    partial = partial.reshape(nseq, -1, partial.shape[1])
+    rows_out, cols_out = partial.shape[0] // nseq, partial.shape[1]
+    partial = partial.reshape(nseq, -1, HEAD_DIMENSION)
     pieces = lax.all_to_all(partial, "seq", 0, 0, tiled=True)
-    projected = jnp.sum(pieces, axis=0).astype(jnp.bfloat16)
+    projected = jnp.sum(pieces, axis=0).reshape(rows_out, cols_out).astype(jnp.bfloat16)
     return (attended, projected)
 
 

time: 62.4 us -> 62.4 us (level)
  no operation moved by 1% of the time
where the time goes in v8:
time: 62.4 us; the launch traced here: 62 us
  blocking collectives  38.8 us (62%)
  starting transfers between devices  7.57 us (12%)
  Pallas kernels  5.56 us (9%)
  waiting for transfers between devices  5.3 us (8%)
  local copies, waits for them, and re-layouts  2.63 us (4%)
  other arithmetic  1.28 us (2%)
  between operations  0.7 us (1%)
    all_to_all x1, blocking collectives, gather_by_all_to_all(): lax.all_to_all(jnp.broadcast_to(x[None], (n,) + x.shape), axis, 0, 0, til...  18.9 us
    all_to_all x1, blocking collectives, body(): parts = lax.all_to_all(packed, 'seq', 0, 0, tiled=True)  10.7 us
    all_to_all x1, blocking collectives, body(): pieces = lax.all_to_all(partial, 'seq', 0, 0, tiled=True)  9.23 us
    all_to_all x1, starting transfers between devices, body(): lax.all_to_all(jnp.broadcast_to(query[:, None, :], (requests, nseq, query...  7.57 us
    pallas_call x1, Pallas kernels, attention(): pl.pallas_call(kernel, grid=(requests,), in_specs=[pl.BlockSpec(memory_sp...  5.56 us
    all_to_all x1, waiting for transfers between devices, body(): lax.all_to_all(jnp.broadcast_to(query[:, None, :], (requests, nseq, query...  5.3 us
    broadcast_in_dim x1, local copies, waits for them, and re-layouts, body(): jnp.broadcast_to(query[:, None, :], (requests, nseq, query.shape[1]))  1.36 us
  transfers between devices with their start and end apart: 1, of which 1 were waited for; matrix products, arithmetic and copies ran while one was open for 2% of the time, Pallas kernels for 0%

profile of v8, /device:TPU:1, one launch (start us, length us, event | category | flops | bytes accessed | tf_op | source)
XLA Modules:
  0.0 62.0 jit_solution(14899976798251707451)
XLA Ops:
  0.6 0.0 copy-start
  0.6 1.4 %broadcast_in_dim.4 = bf16[2,16,512]{2,0,1:T(2,128)(2,1)} broadcast(bf16[2,512]{1,0:T(2,128)(2,1)} %param.6), dimensions={0,2} | broadcast | bytes 34816 | tf_op jit(solution)/shard_map/broadcast_in_dim | solution.py:101
  2.0 7.6 %all-to-all-start = ((bf16[2,16,512]{2,0,1:T(2,128)(2,1)}), bf16[2,16,512]{2,0,1:T(2,128)(2,1)S(1)}, u32[]{:S(2)}, u32[]{:S(2)}) async-start(bf16[2,16,512]{2,0,1:T(2,128)(2,1)} %broadcast_in_dim.4), calls=%async_computation | async-start | bytes 65536 | tf_op jit(solution)/shard_map/all_to_all | solution.py:100
  9.6 1.2 %broadcast_subtract_fusion.lim_ref = s32[2]{0:T(128)} fusion(s32[2]{0:T(128)} %param.10, s32[]{:T(128)S(6)} %mul.12), kind=kLoop, calls=%fused_computation.9 | loop fusion | flops 2 | bytes 20 | tf_op jit(solution)/shard_map/sub | solution.py:104
  10.8 5.3 %all-to-all-done = bf16[2,16,512]{2,0,1:T(2,128)(2,1)S(1)} async-done(((bf16[2,16,512]{2,0,1:T(2,128)(2,1)}), bf16[2,16,512]{2,0,1:T(2,128)(2,1)S(1)}, u32[]{:S(2)}, u32[]{:S(2)}) %all-to-all-start) | async-done | bytes 32800 | tf_op jit(solution)/shard_map/all_to_all | solution.py:100
  16.1 0.6 copy.8.h_ref
  16.7 5.6 %shard_map.77 = f32[16,2,4,384]{3,2,1,0:T(4,128)} custom-call(s32[2,32]{1,0:T(2,128)} %sel_ref.1, s32[2]{0:T(128)} %broadcast_subtract_fusion.lim_ref, s32[1]{0:T(128)} %bitcast.base_ref, bf16[2,16,512]{2,1,0:T(8,128)(2,1)} %copy.8.h_ref, bf16[2,1024,1024]{2,1,0:T(8,128)(2,1)} %k_ref.1, bf16[2,1024,1024]{2,1,0:T(8,128)(2,1)} %v_ref.1), custom_call_target="tpu_custom_call" | custom-call | flops 536870912 | bytes 8421376 | tf_op jit(solution)/shard_map/pallas_call | solution.py:69
  22.2 10.7 %all_to_all.20 = f32[16,2,4,384]{3,2,1,0:T(4,128)S(1)} all-to-all(f32[16,2,4,384]{3,2,1,0:T(4,128)} %shard_map.77), channel_id=1, replica_groups=mesh['grp'=16,'seq'=16] {'seq'}, dimensions={0} | all-to-all | bytes 393216 | tf_op jit(solution)/shard_map/all_to_all | solution.py:107
  32.9 0.1 fusion
  33.0 0.0 copy-start.1
  33.0 18.9 %all_to_all.21 = bf16[16,2,512]{2,1,0:T(2,128)(2,1)S(1)} all-to-all(bf16[16,2,512]{2,1,0:T(2,128)(2,1)S(1)} %broadcast_in_dim.5), channel_id=1, replica_groups=mesh['grp'=16,'seq'=16] {'grp'}, dimensions={0} | all-to-all | bytes 65536 | tf_op jit(solution)/shard_map/all_to_all | solution.py:19
  52.0 0.0 copy-done
  52.0 0.2 fusion.3
  52.2 9.2 %all_to_all.22 = f32[16,8,128]{2,1,0:T(8,128)S(1)} all-to-all(f32[16,8,128]{2,1,0:T(8,128)S(1)} %reshape.34), channel_id=1, replica_groups=mesh['grp'=16,'seq'=16] {'seq'}, dimensions={0} | all-to-all | bytes 131072 | tf_op jit(solution)/shard_map/all_to_all | solution.py:124
  61.4 0.6 convert_element_type.19
  62.0 0.0 copy-done.1
  (7 shorter events, 0.1 us)
Async XLA Ops:
  0.6 51.3 %copy-start = (bf16[512,512]{1,0:T(8,128)(2,1)S(1)}, bf16[512,512]{1,0:T(8,128)(2,1)}, u32[]{:S(2)}) copy-start(bf16[512,512]{1,0:T(8,128)(2,1)} %param.11) | copy-start | bytes 1572868
  2.0 14.1 %all-to-all-start = ((bf16[2,16,512]{2,0,1:T(2,128)(2,1)}), bf16[2,16,512]{2,0,1:T(2,128)(2,1)S(1)}, u32[]{:S(2)}, u32[]{:S(2)}) async-start(bf16[2,16,512]{2,0,1:T(2,128)(2,1)} %broadcast_in_dim.4), calls=%async_computation | async-start | bytes 65536 | tf_op jit(solution)/shard_map/all_to_all | solution.py:100
  33.0 29.0 %copy-start.1 = (bf16[1,2,4,128]{3,1,2,0:T(2,128)(2,1)}, bf16[1,2,4,128]{3,1,2,0:T(2,128)(2,1)S(1)}, u32[]{:S(2)}) copy-start(bf16[1,2,4,128]{3,1,2,0:T(2,128)(2,1)S(1)} %copy.11) | copy-start | bytes 6148

commit v9 on v8

--- a/solution.py
+++ b/solution.py
@@ -22,24 +22,32 @@
 def attention_kernel(sel_ref, lim_ref, base_ref, h_ref, k_ref, v_ref, out_ref, qd_ref, *, scale, head_group):
     _, nseq, local_width = h_ref.shape
     heads_dev = local_width // HEAD_DIMENSION
-    q_heads = nseq * heads_dev
-    qd_ref[...] = jnp.zeros(qd_ref.shape, qd_ref.dtype)
-    for src in range(nseq):
-        for i in range(heads_dev):
-            h = src * heads_dev + i
-            kv = h // head_group
-            qd_ref[h:h + 1, kv * HEAD_DIMENSION:(kv + 1) * HEAD_DIMENSION] = h_ref[
-                0, src:src + 1, i * HEAD_DIMENSION:(i + 1) * HEAD_DIMENSION
-            ].astype(qd_ref.dtype)
-    q = qd_ref[...].astype(jnp.bfloat16)
+    tok, cols = k_ref.shape[1:]
+    kv_step = cols // HEAD_DIMENSION
+    heads_step = kv_step * head_group
+    src_step = heads_step // heads_dev
     r = pl.program_id(0)
-    tok = k_ref.shape[1]
+    c = pl.program_id(1)
     lane = lax.broadcasted_iota(jnp.int32, (1, tok), 1)
     page = base_ref[0] + lane // PAGE
     picked = page == sel_ref[r, 0]
     for j in range(1, sel_ref.shape[1]):
         picked = picked | (page == sel_ref[r, j])
     live = picked & (lane < lim_ref[r])
+    for chunk in range(nseq // src_step):
+        @pl.when(c == chunk)
+        def _():
+            qd_ref[...] = jnp.zeros(qd_ref.shape, qd_ref.dtype)
+            for s_local in range(src_step):
+                src = chunk * src_step + s_local
+                for i in range(heads_dev):
+                    h = s_local * heads_dev + i
+                    kv = h // head_group
+                    qd_ref[h:h + 1, kv * HEAD_DIMENSION:(kv + 1) * HEAD_DIMENSION] = h_ref[
+                        0, src:src + 1, i * HEAD_DIMENSION:(i + 1) * HEAD_DIMENSION
+                    ].astype(qd_ref.dtype)
+
+    q = qd_ref[...].astype(jnp.bfloat16)
     scores = lax.dot_general(
         q, k_ref[0], (((1,), (1,)), ((), ())), preferred_element_type=jnp.float32
     ) * scale
@@ -48,9 +56,9 @@
     weights = jnp.where(live, jnp.exp(scores - peak), 0.0)
     total = jnp.sum(weights, axis=-1, keepdims=True)
     full = jnp.dot(weights.astype(jnp.bfloat16), v_ref[0], preferred_element_type=jnp.float32)
-    peak_lanes = jnp.broadcast_to(peak, (q_heads, HEAD_DIMENSION))
-    total_lanes = jnp.broadcast_to(total, (q_heads, HEAD_DIMENSION))
-    for d in range(nseq):
+    peak_lanes = jnp.broadcast_to(peak, (heads_step, HEAD_DIMENSION))
+    total_lanes = jnp.broadcast_to(total, (heads_step, HEAD_DIMENSION))
+    for d in range(src_step):
         rows = slice(d * heads_dev, (d + 1) * heads_dev)
         kv = d * heads_dev // head_group
         out_ref[d, 0, :, 0:HEAD_DIMENSION] = full[rows, kv * HEAD_DIMENSION:(kv + 1) * HEAD_DIMENSION]
@@ -58,28 +66,32 @@
         out_ref[d, 0, :, 2 * HEAD_DIMENSION:] = total_lanes[rows, :]
 
 
-def attention(heads_all, selected, limit, base, key_cache, value_store_cache, scale, head_group):
+def attention(heads_all, selected, limit, base, key_cache, value_store_cache, scale, head_group, steps=2):
     requests, nseq, local_width = heads_all.shape
     heads_dev = local_width // HEAD_DIMENSION
     q_heads = nseq * heads_dev
     tok, width = key_cache.shape[1:]
+    cols = width // steps
+    heads_step = q_heads // steps
+    src_step = nseq // steps
     kernel = functools.partial(attention_kernel, scale=scale, head_group=head_group)
-    flops = 4 * requests * q_heads * tok * width
+    flops = 4 * requests * q_heads * tok * cols
     nbytes = 2 * (key_cache.size + value_store_cache.size + heads_all.size)
+    smem = pl.BlockSpec(memory_space=pltpu.SMEM)
     return pl.pallas_call(
         kernel,
-        grid=(requests,),
+        grid=(requests, steps),
         in_specs=[
-            pl.BlockSpec(memory_space=pltpu.SMEM),
-            pl.BlockSpec(memory_space=pltpu.SMEM),
-            pl.BlockSpec(memory_space=pltpu.SMEM),
-            pl.BlockSpec((1, nseq, local_width), lambda r: (r, 0, 0)),
-            pl.BlockSpec((1, tok, width), lambda r: (r, 0, 0)),
-            pl.BlockSpec((1, tok, width), lambda r: (r, 0, 0)),
+            smem,
+            smem,
+            smem,
+            pl.BlockSpec((1, nseq, local_width), lambda r, c: (r, 0, 0)),
+            pl.BlockSpec((1, tok, cols), lambda r, c: (r, 0, c)),
+            pl.BlockSpec((1, tok, cols), lambda r, c: (r, 0, c)),
         ],
-        out_specs=pl.BlockSpec((nseq, 1, heads_dev, 3 * HEAD_DIMENSION), lambda r: (0, r, 0, 0)),
+        out_specs=pl.BlockSpec((src_step, 1, heads_dev, 3 * HEAD_DIMENSION), lambda r, c: (c, r, 0, 0)),
         out_shape=jax.ShapeDtypeStruct((nseq, requests, heads_dev, 3 * HEAD_DIMENSION), jnp.float32),
-        scratch_shapes=[pltpu.VMEM((q_heads, width), jnp.float32)],
+        scratch_shapes=[pltpu.VMEM((heads_step, cols), jnp.float32)],
         cost_estimate=pl.CostEstimate(
             flops=flops, transcendentals=requests * q_heads * tok, bytes_accessed=nbytes
         ),

time: 62.4 us -> 63.5 us (1.018)
  Pallas kernels: 5.56 us -> 6.65 us
    pallas_call x1, Pallas kernels: 5.56 us -> 6.65 us  [attention(): pl.pallas_call(kernel, grid=(requests, steps), in_specs=[smem, smem, smem...]
where the time goes in v9:
time: 63.5 us; the launch traced here: 63.1 us
  blocking collectives  38.8 us (61%)
  starting transfers between devices  7.57 us (12%)
  Pallas kernels  6.65 us (10%)
  waiting for transfers between devices  5.3 us (8%)
  local copies, waits for them, and re-layouts  2.63 us (4%)
  other arithmetic  1.28 us (2%)
  between operations  0.7 us (1%)
    all_to_all x1, blocking collectives, gather_by_all_to_all(): lax.all_to_all(jnp.broadcast_to(x[None], (n,) + x.shape), axis, 0, 0, til...  18.9 us
    all_to_all x1, blocking collectives, body(): parts = lax.all_to_all(packed, 'seq', 0, 0, tiled=True)  10.7 us
    all_to_all x1, blocking collectives, body(): pieces = lax.all_to_all(partial, 'seq', 0, 0, tiled=True)  9.23 us
    all_to_all x1, starting transfers between devices, body(): lax.all_to_all(jnp.broadcast_to(query[:, None, :], (requests, nseq, query...  7.57 us
    pallas_call x1, Pallas kernels, attention(): pl.pallas_call(kernel, grid=(requests, steps), in_specs=[smem, smem, smem...  6.65 us
    all_to_all x1, waiting for transfers between devices, body(): lax.all_to_all(jnp.broadcast_to(query[:, None, :], (requests, nseq, query...  5.3 us
    broadcast_in_dim x1, local copies, waits for them, and re-layouts, body(): jnp.broadcast_to(query[:, None, :], (requests, nseq, query.shape[1]))  1.36 us
  transfers between devices with their start and end apart: 1, of which 1 were waited for; matrix products, arithmetic and copies ran while one was open for 2% of the time, Pallas kernels for 0%

profile of v9, /device:TPU:1, one launch (start us, length us, event | category | flops | bytes accessed | tf_op | source)
XLA Modules:
  0.0 63.1 jit_solution(14033857905569282624)
XLA Ops:
  0.6 0.0 copy-start
  0.6 1.4 %broadcast_in_dim.4 = bf16[2,16,512]{2,0,1:T(2,128)(2,1)} broadcast(bf16[2,512]{1,0:T(2,128)(2,1)} %param.6), dimensions={0,2} | broadcast | bytes 34816 | tf_op jit(solution)/shard_map/broadcast_in_dim | solution.py:113
  2.0 7.6 %all-to-all-start = ((bf16[2,16,512]{2,0,1:T(2,128)(2,1)}), bf16[2,16,512]{2,0,1:T(2,128)(2,1)S(1)}, u32[]{:S(2)}, u32[]{:S(2)}) async-start(bf16[2,16,512]{2,0,1:T(2,128)(2,1)} %broadcast_in_dim.4), calls=%async_computation | async-start | bytes 65536 | tf_op jit(solution)/shard_map/all_to_all | solution.py:112
  9.6 1.2 %broadcast_subtract_fusion.lim_ref = s32[2]{0:T(128)} fusion(s32[2]{0:T(128)} %param.10, s32[]{:T(128)S(6)} %mul.12), kind=kLoop, calls=%fused_computation.9 | loop fusion | flops 2 | bytes 20 | tf_op jit(solution)/shard_map/sub | solution.py:116
  10.8 5.3 %all-to-all-done = bf16[2,16,512]{2,0,1:T(2,128)(2,1)S(1)} async-done(((bf16[2,16,512]{2,0,1:T(2,128)(2,1)}), bf16[2,16,512]{2,0,1:T(2,128)(2,1)S(1)}, u32[]{:S(2)}, u32[]{:S(2)}) %all-to-all-start) | async-done | bytes 32800 | tf_op jit(solution)/shard_map/all_to_all | solution.py:112
  16.1 0.6 copy.8.h_ref
  16.7 6.7 %shard_map.77 = f32[16,2,4,384]{3,2,1,0:T(4,128)} custom-call(s32[2,32]{1,0:T(2,128)} %sel_ref.1, s32[2]{0:T(128)} %broadcast_subtract_fusion.lim_ref, s32[1]{0:T(128)} %bitcast.base_ref, bf16[2,16,512]{2,1,0:T(8,128)(2,1)} %copy.8.h_ref, bf16[2,1024,1024]{2,1,0:T(8,128)(2,1)} %k_ref.1, bf16[2,1024,1024]{2,1,0:T(8,128)(2,1)} %v_ref.1), custom_call_target="tpu_custom_call" | custom-call | flops 268435456 | bytes 8421376 | tf_op jit(solution)/shard_map/pallas_call | solution.py:81
  23.3 10.7 %all_to_all.20 = f32[16,2,4,384]{3,2,1,0:T(4,128)S(1)} all-to-all(f32[16,2,4,384]{3,2,1,0:T(4,128)} %shard_map.77), channel_id=1, replica_groups=mesh['grp'=16,'seq'=16] {'seq'}, dimensions={0} | all-to-all | bytes 393216 | tf_op jit(solution)/shard_map/all_to_all | solution.py:119
  34.0 0.1 fusion
  34.1 0.0 copy-start.1
  34.1 18.9 %all_to_all.21 = bf16[16,2,512]{2,1,0:T(2,128)(2,1)S(1)} all-to-all(bf16[16,2,512]{2,1,0:T(2,128)(2,1)S(1)} %broadcast_in_dim.5), channel_id=1, replica_groups=mesh['grp'=16,'seq'=16] {'grp'}, dimensions={0} | all-to-all | bytes 65536 | tf_op jit(solution)/shard_map/all_to_all | solution.py:19
  53.0 0.0 copy-done
  53.1 0.2 fusion.3
  53.3 9.2 %all_to_all.22 = f32[16,8,128]{2,1,0:T(8,128)S(1)} all-to-all(f32[16,8,128]{2,1,0:T(8,128)S(1)} %reshape.34), channel_id=1, replica_groups=mesh['grp'=16,'seq'=16] {'seq'}, dimensions={0} | all-to-all | bytes 131072 | tf_op jit(solution)/shard_map/all_to_all | solution.py:136
  62.5 0.6 convert_element_type.19
  63.1 0.0 copy-done.1
  (7 shorter events, 0.1 us)
Async XLA Ops:
  0.6 52.4 %copy-start = (bf16[512,512]{1,0:T(8,128)(2,1)S(1)}, bf16[512,512]{1,0:T(8,128)(2,1)}, u32[]{:S(2)}) copy-start(bf16[512,512]{1,0:T(8,128)(2,1)} %param.11) | copy-start | bytes 1572868
  2.0 14.1 %all-to-all-start = ((bf16[2,16,512]{2,0,1:T(2,128)(2,1)}), bf16[2,16,512]{2,0,1:T(2,128)(2,1)S(1)}, u32[]{:S(2)}, u32[]{:S(2)}) async-start(bf16[2,16,512]{2,0,1:T(2,128)(2,1)} %broadcast_in_dim.4), calls=%async_computation | async-start | bytes 65536 | tf_op jit(solution)/shard_map/all_to_all | solution.py:112
  34.1 29.0 %copy-start.1 = (bf16[1,2,4,128]{3,1,2,0:T(2,128)(2,1)}, bf16[1,2,4,128]{3,1,2,0:T(2,128)(2,1)S(1)}, u32[]{:S(2)}) copy-start(bf16[1,2,4,128]{3,1,2,0:T(2,128)(2,1)S(1)} %copy.11) | copy-start | bytes 6148

commit v10 on v8

--- a/solution.py
+++ b/solution.py
@@ -48,14 +48,14 @@
     weights = jnp.where(live, jnp.exp(scores - peak), 0.0)
     total = jnp.sum(weights, axis=-1, keepdims=True)
     full = jnp.dot(weights.astype(jnp.bfloat16), v_ref[0], preferred_element_type=jnp.float32)
-    peak_lanes = jnp.broadcast_to(peak, (q_heads, HEAD_DIMENSION))
-    total_lanes = jnp.broadcast_to(total, (q_heads, HEAD_DIMENSION))
+    half = HEAD_DIMENSION // 2
+    stat_lane = lax.broadcasted_iota(jnp.int32, (q_heads, HEAD_DIMENSION), 1)
+    stat = jnp.where(stat_lane < half, peak, total)
     for d in range(nseq):
         rows = slice(d * heads_dev, (d + 1) * heads_dev)
         kv = d * heads_dev // head_group
         out_ref[d, 0, :, 0:HEAD_DIMENSION] = full[rows, kv * HEAD_DIMENSION:(kv + 1) * HEAD_DIMENSION]
-        out_ref[d, 0, :, HEAD_DIMENSION:2 * HEAD_DIMENSION] = peak_lanes[rows, :]
-        out_ref[d, 0, :, 2 * HEAD_DIMENSION:] = total_lanes[rows, :]
+        out_ref[d, 0, :, HEAD_DIMENSION:] = stat[rows, :]
 
 
 def attention(heads_all, selected, limit, base, key_cache, value_store_cache, scale, head_group):
@@ -77,8 +77,8 @@
             pl.BlockSpec((1, tok, width), lambda r: (r, 0, 0)),
             pl.BlockSpec((1, tok, width), lambda r: (r, 0, 0)),
         ],
-        out_specs=pl.BlockSpec((nseq, 1, heads_dev, 3 * HEAD_DIMENSION), lambda r: (0, r, 0, 0)),
-        out_shape=jax.ShapeDtypeStruct((nseq, requests, heads_dev, 3 * HEAD_DIMENSION), jnp.float32),
+        out_specs=pl.BlockSpec((nseq, 1, heads_dev, 2 * HEAD_DIMENSION), lambda r: (0, r, 0, 0)),
+        out_shape=jax.ShapeDtypeStruct((nseq, requests, heads_dev, 2 * HEAD_DIMENSION), jnp.float32),
         scratch_shapes=[pltpu.VMEM((q_heads, width), jnp.float32)],
         cost_estimate=pl.CostEstimate(
             flops=flops, transcendentals=requests * q_heads * tok, bytes_accessed=nbytes
@@ -105,13 +105,15 @@
     base = jnp.reshape(me * (tok_local // PAGE), (1,)).astype(jnp.int32)
     packed = attention(heads_all, selected, limit, base, key_cache, value_store_cache, scale, head_group)
     parts = lax.all_to_all(packed, "seq", 0, 0, tiled=True)
+    half = HEAD_DIMENSION // 2
     b_out = parts[..., :HEAD_DIMENSION]
-    b_max = parts[..., HEAD_DIMENSION:2 * HEAD_DIMENSION]
-    b_sum = parts[..., 2 * HEAD_DIMENSION:]
+    b_max = parts[..., HEAD_DIMENSION:HEAD_DIMENSION + half]
+    b_sum = parts[..., HEAD_DIMENSION + half:]
     top = jnp.max(b_max, axis=0)
     factor = jnp.exp(b_max - top[None])
     whole_total = jnp.sum(b_sum * factor, axis=0)
-    whole_accum = jnp.sum(b_out * factor, axis=0)
+    whole_total = jnp.concatenate([whole_total, whole_total], axis=-1)
+    whole_accum = jnp.sum(b_out * jnp.concatenate([factor, factor], axis=-1), axis=0)
     attended = (
         (whole_accum / whole_total)
         .reshape(requests, heads_dev * HEAD_DIMENSION)

time: 62.4 us -> 62.3 us (level)
  no operation moved by 1% of the time
where the time goes in v10:
time: 62.3 us; the launch traced here: 61.9 us
  blocking collectives  38.5 us (62%)
  starting transfers between devices  7.57 us (12%)
  Pallas kernels  5.52 us (9%)
  waiting for transfers between devices  5.3 us (9%)
  local copies, waits for them, and re-layouts  2.63 us (4%)
  other arithmetic  1.52 us (2%)
  between operations  0.7 us (1%)
    all_to_all x1, blocking collectives, gather_by_all_to_all(): lax.all_to_all(jnp.broadcast_to(x[None], (n,) + x.shape), axis, 0, 0, til...  18.9 us
    all_to_all x1, blocking collectives, body(): parts = lax.all_to_all(packed, 'seq', 0, 0, tiled=True)  10.3 us
    all_to_all x1, blocking collectives, body(): pieces = lax.all_to_all(partial, 'seq', 0, 0, tiled=True)  9.32 us
    all_to_all x1, starting transfers between devices, body(): lax.all_to_all(jnp.broadcast_to(query[:, None, :], (requests, nseq, query...  7.57 us
    pallas_call x1, Pallas kernels, attention(): pl.pallas_call(kernel, grid=(requests,), in_specs=[pl.BlockSpec(memory_sp...  5.52 us
    all_to_all x1, waiting for transfers between devices, body(): lax.all_to_all(jnp.broadcast_to(query[:, None, :], (requests, nseq, query...  5.3 us
    broadcast_in_dim x1, local copies, waits for them, and re-layouts, body(): jnp.broadcast_to(query[:, None, :], (requests, nseq, query.shape[1]))  1.36 us
  transfers between devices with their start and end apart: 1, of which 1 were waited for; matrix products, arithmetic and copies ran while one was open for 2% of the time, Pallas kernels for 0%

profile of v10, /device:TPU:1, one launch (start us, length us, event | category | flops | bytes accessed | tf_op | source)
XLA Modules:
  0.0 61.9 jit_solution(9509261502161905114)
XLA Ops:
  0.6 0.0 copy-start
  0.6 1.4 %broadcast_in_dim.4 = bf16[2,16,512]{2,0,1:T(2,128)(2,1)} broadcast(bf16[2,512]{1,0:T(2,128)(2,1)} %param.6), dimensions={0,2} | broadcast | bytes 34816 | tf_op jit(solution)/shard_map/broadcast_in_dim | solution.py:101
  2.0 7.6 %all-to-all-start = ((bf16[2,16,512]{2,0,1:T(2,128)(2,1)}), bf16[2,16,512]{2,0,1:T(2,128)(2,1)S(1)}, u32[]{:S(2)}, u32[]{:S(2)}) async-start(bf16[2,16,512]{2,0,1:T(2,128)(2,1)} %broadcast_in_dim.4), calls=%async_computation | async-start | bytes 65536 | tf_op jit(solution)/shard_map/all_to_all | solution.py:100
  9.6 1.2 %broadcast_subtract_fusion.lim_ref = s32[2]{0:T(128)} fusion(s32[2]{0:T(128)} %param.10, s32[]{:T(128)S(6)} %mul.12), kind=kLoop, calls=%fused_computation.10 | loop fusion | flops 2 | bytes 20 | tf_op jit(solution)/shard_map/sub | solution.py:104
  10.8 5.3 %all-to-all-done = bf16[2,16,512]{2,0,1:T(2,128)(2,1)S(1)} async-done(((bf16[2,16,512]{2,0,1:T(2,128)(2,1)}), bf16[2,16,512]{2,0,1:T(2,128)(2,1)S(1)}, u32[]{:S(2)}, u32[]{:S(2)}) %all-to-all-start) | async-done | bytes 32800 | tf_op jit(solution)/shard_map/all_to_all | solution.py:100
  16.1 0.6 copy.8.h_ref
  16.7 5.5 %shard_map.77 = f32[16,2,4,256]{3,2,1,0:T(4,128)} custom-call(s32[2,32]{1,0:T(2,128)} %sel_ref.1, s32[2]{0:T(128)} %broadcast_subtract_fusion.lim_ref, s32[1]{0:T(128)} %bitcast.base_ref, bf16[2,16,512]{2,1,0:T(8,128)(2,1)} %copy.8.h_ref, bf16[2,1024,1024]{2,1,0:T(8,128)(2,1)} %k_ref.1, bf16[2,1024,1024]{2,1,0:T(8,128)(2,1)} %v_ref.1), custom_call_target="tpu_custom_call" | custom-call | flops 536870912 | bytes 8421376 | tf_op jit(solution)/shard_map/pallas_call | solution.py:69
  22.2 10.3 %all_to_all.20 = f32[16,2,4,256]{3,2,1,0:T(4,128)S(1)} all-to-all(f32[16,2,4,256]{3,2,1,0:T(4,128)} %shard_map.77), channel_id=1, replica_groups=mesh['grp'=16,'seq'=16] {'seq'}, dimensions={0} | all-to-all | bytes 262144 | tf_op jit(solution)/shard_map/all_to_all | solution.py:107
  32.5 0.1 fusion
  32.6 0.1 fusion.1
  32.7 0.1 fusion.3
  32.8 0.0 copy-start.1
  32.9 18.9 %all_to_all.21 = bf16[16,2,512]{2,1,0:T(2,128)(2,1)S(1)} all-to-all(bf16[16,2,512]{2,1,0:T(2,128)(2,1)S(1)} %broadcast_in_dim.5), channel_id=1, replica_groups=mesh['grp'=16,'seq'=16] {'grp'}, dimensions={0} | all-to-all | bytes 65536 | tf_op jit(solution)/shard_map/all_to_all | solution.py:19
  51.8 0.0 copy-done
  51.8 0.2 fusion.4
  52.0 9.3 %all_to_all.22 = f32[16,8,128]{2,1,0:T(8,128)S(1)} all-to-all(f32[16,8,128]{2,1,0:T(8,128)S(1)} %reshape.34), channel_id=1, replica_groups=mesh['grp'=16,'seq'=16] {'seq'}, dimensions={0} | all-to-all | bytes 131072 | tf_op jit(solution)/shard_map/all_to_all | solution.py:126
  61.3 0.6 convert_element_type.19
  61.9 0.0 copy-done.1
  (6 shorter events, 0.1 us)
Async XLA Ops:
  0.6 51.2 %copy-start = (bf16[512,512]{1,0:T(8,128)(2,1)S(1)}, bf16[512,512]{1,0:T(8,128)(2,1)}, u32[]{:S(2)}) copy-start(bf16[512,512]{1,0:T(8,128)(2,1)} %param.11) | copy-start | bytes 1572868
  2.0 14.1 %all-to-all-start = ((bf16[2,16,512]{2,0,1:T(2,128)(2,1)}), bf16[2,16,512]{2,0,1:T(2,128)(2,1)S(1)}, u32[]{:S(2)}, u32[]{:S(2)}) async-start(bf16[2,16,512]{2,0,1:T(2,128)(2,1)} %broadcast_in_dim.4), calls=%async_computation | async-start | bytes 65536 | tf_op jit(solution)/shard_map/all_to_all | solution.py:100
  32.8 29.1 %copy-start.1 = (bf16[1,2,4,128]{3,1,2,0:T(2,128)(2,1)}, bf16[1,2,4,128]{3,1,2,0:T(2,128)(2,1)S(1)}, u32[]{:S(2)}) copy-start(bf16[1,2,4,128]{3,1,2,0:T(2,128)(2,1)S(1)} %copy.11) | copy-start | bytes 6148
